TPU v7x, 128 devices: a whole 4x4x4 slice. The times are simulated.
128 devices in a mesh: req: 16 (over y, z), mp: 8 (over x, core).
Axes of the slice: x: 4, y: 4, z: 4, core: 2. Of those that a mesh axis runs over, the one named last changes fastest.
Arguments:
- hidden_in: bfloat16 [16384, 2048], P('req', 'mp'), may hold values from -6 to 6
- w_qkv: bfloat16 [3, 2048, 2048], P(None, 'req', 'mp'), may hold values from -0.125 to 0.125
- w_out: bfloat16 [2048, 2048], P('mp', 'req'), may hold values from -0.125 to 0.125
- attn_gain: bfloat16 [2048], replicated, may hold values from 0.099609375 to 1.8984375
- mlp_gain: bfloat16 [2048], replicated, may hold values from 0.099609375 to 1.8984375
- w_gate: bfloat16 [2048, 8192], P('req', 'mp'), may hold values from -0.125 to 0.125
- w_up: bfloat16 [2048, 8192], P('req', 'mp'), may hold values from -0.125 to 0.125
- w_down: bfloat16 [8192, 2048], P('mp', 'req'), may hold values from -0.0625 to 0.0625
- k_cache: bfloat16 [16, 4096, 2048], P('req', None, 'mp'), may hold values from -363 to 363
- v_cache: bfloat16 [16, 4096, 2048], P('req', None, 'mp'), may hold values from -6 to 6
- cache_len: int32 [16], P('req'), may hold values from 256 to 4096, as said below
Outputs:
- hidden_out: bfloat16 [16384, 2048], P('req', 'mp')
- new_keys: bfloat16 [16384, 2048], P('req', 'mp')
- new_values: bfloat16 [16384, 2048], P('req', 'mp')
Inputs may be any that keep to these rules, and one draw needn't show every extreme that they name: Each request uses its first cache_len slots; later slots hold unused data. Some request's cache is full in every draw.
All inputs are finite; a program needn't handle non-finite values.
Results may differ from a plain program's by a relative error of at most 0.02.
Values may be sent and summed in bfloat16 or wider, within the bound.
No kernel may reach another device: no remote copies, remote signals or barrier semaphores. Data moves between devices by JAX's collectives and lax.ppermute only.
A program may use at most 128 MiB of HBM per device.

v0:
```python
import jax
import jax.numpy as jnp
from jax import lax
from jax.sharding import PartitionSpec as P
from jax.experimental import pallas as pl
from jax.experimental.pallas import tpu as pltpu
import functools

HD = 64


THETA = 130000.0
EPSILON = 1e-05
NEG_FILL = -1e30


def rms_scale(rows, gain):
    values = rows.astype(jnp.float32)
    meansq = jnp.mean(values * values, axis=-1, keepdims=True)
    return (values * lax.rsqrt(meansq + EPSILON) * gain.astype(jnp.float32)).astype(jnp.bfloat16)


def gather_req_shifted(block, axis, axis_name):
    count = lax.axis_size(axis_name)
    side = int(round(count ** 0.5))
    me = lax.axis_index(axis_name)
    row, col = me // side, me % side

    def inner(k):
        return [(s, (s // side) * side + (s % side - k) % side) for s in range(count)]

    def outer(k):
        return [(s, ((s // side - k) % side) * side + s % side) for s in range(count)]

    parts = [block] + [lax.ppermute(block, axis_name, inner(k)) for k in range(1, side)]
    stage = jnp.stack(parts, axis=axis)
    parts = [stage] + [lax.ppermute(stage, axis_name, outer(k)) for k in range(1, side)]
    return jnp.stack(parts, axis=axis), row, col


def gather_packed(blocks, axes, axis_name):
    count = lax.axis_size(axis_name)
    lane = 128
    joined = jnp.concatenate([block.reshape(-1, lane) for block in blocks], axis=0)
    gathered = lax.all_gather(joined, axis_name, axis=0, tiled=False)
    outs = []
    offset = 0
    for block, axis in zip(blocks, axes):
        rows = block.size // lane
        piece = gathered[:, offset:offset + rows].reshape((count,) + block.shape)
        piece = jnp.moveaxis(piece, 0, axis)
        shape = list(block.shape)
        shape[axis] *= count
        outs.append(piece.reshape(shape))
        offset += rows
    return outs


def flash_body(len_ref, q_ref, kc_ref, vc_ref, kn_ref, vn_ref, o_ref, m_sc, l_sc, acc_sc, *, tk, n_cache, scale):
    j = pl.program_id(1)
    length = len_ref[0]
    tq = q_ref.shape[1]

    @pl.when(j == 0)
    def _():
        m_sc[...] = jnp.full(m_sc.shape, NEG_FILL, jnp.float32)
        l_sc[...] = jnp.zeros(l_sc.shape, jnp.float32)
        acc_sc[...] = jnp.zeros(acc_sc.shape, jnp.float32)

    def update(k, v, mask):
        s = lax.dot_general(q_ref[0] * scale, k, (((1,), (1,)), ((), ())), preferred_element_type=jnp.float32)
        if mask is not None:
            s = jnp.where(mask, s, NEG_FILL)
        m_prev = m_sc[...]
        m_new = jnp.maximum(m_prev, jnp.max(s, axis=1, keepdims=True))
        alpha = jnp.exp(m_prev - m_new)
        p = jnp.exp(s - m_new)
        if mask is not None:
            p = jnp.where(mask, p, 0.0)
        l_sc[...] = alpha * l_sc[...] + jnp.sum(p, axis=1, keepdims=True)
        acc_sc[...] = alpha * acc_sc[...] + jnp.dot(p.astype(jnp.bfloat16), v, preferred_element_type=jnp.float32)
        m_sc[...] = m_new

    begin = j * tk

    @pl.when((j < n_cache) & (begin + tk <= length))
    def _():
        update(kc_ref[0], vc_ref[0], None)

    @pl.when((j < n_cache) & (begin < length) & (begin + tk > length))
    def _():
        col = begin + lax.broadcasted_iota(jnp.int32, (tq, tk), 1)
        update(kc_ref[0], vc_ref[0], col < length)

    @pl.when(j == n_cache)
    def _():
        row = lax.broadcasted_iota(jnp.int32, (tq, tq), 0)
        col = lax.broadcasted_iota(jnp.int32, (tq, tq), 1)
        update(kn_ref[0], vn_ref[0], row >= col)
        o_ref[0] = (acc_sc[...] / l_sc[...]).astype(o_ref.dtype)


def flash_attention(length, q, kc, vc, kn, vn):
    heads, new_count, hd = q.shape
    slots = kc.shape[1]
    tk = min(new_count, slots)
    n_cache = slots // tk
    body = functools.partial(flash_body, tk=tk, n_cache=n_cache, scale=hd ** (-0.5))

    def cache_map(h, j, len_ref):
        last = jnp.maximum(len_ref[0] - 1, 0) // tk
        return (h, jnp.minimum(j, last), 0)

    fixed = lambda h, j, len_ref: (h, 0, 0)
    grid_spec = pltpu.PrefetchScalarGridSpec(
        num_scalar_prefetch=1,
        grid=(heads, n_cache + 1),
        in_specs=[
            pl.BlockSpec((1, new_count, hd), fixed),
            pl.BlockSpec((1, tk, hd), cache_map),
            pl.BlockSpec((1, tk, hd), cache_map),
            pl.BlockSpec((1, new_count, hd), fixed),
            pl.BlockSpec((1, new_count, hd), fixed),
        ],
        out_specs=pl.BlockSpec((1, new_count, hd), fixed),
        scratch_shapes=[
            pltpu.VMEM((new_count, 1), jnp.float32),
            pltpu.VMEM((new_count, 1), jnp.float32),
            pltpu.VMEM((new_count, hd), jnp.float32),
        ],
    )
    flops = 4 * heads * new_count * (slots + new_count) * hd
    cost = pl.CostEstimate(
        flops=flops,
        transcendentals=heads * new_count * (slots + new_count),
        bytes_accessed=2 * (q.size + kc.size + vc.size + kn.size + vn.size) + 4 * q.size,
    )
    return pl.pallas_call(
        body,
        grid_spec=grid_spec,
        out_shape=jax.ShapeDtypeStruct((heads, new_count, hd), jnp.bfloat16),
        compiler_params=pltpu.CompilerParams(
            dimension_semantics=("arbitrary", "arbitrary"), vmem_limit_bytes=56 * 1024 * 1024
        ),
        cost_estimate=cost,
    )(length, q, kc, vc, kn, vn)


def on_device(
    hidden_in, w_qkv, w_out, attn_gain, mlp_gain, w_gate, w_up, w_down, k_cache, v_cache, cache_len
):
    new_count = hidden_in.shape[0]
    qkv_shifted, row, col = gather_req_shifted(w_qkv, 1, "req")
    side = qkv_shifted.shape[1]
    w_qkv_full = qkv_shifted.reshape(3, -1, w_qkv.shape[2])
    w_gate_full, w_up_full, w_down_full, w_out_full = gather_packed(
        [w_gate, w_up, w_down, w_out], [0, 0, 1, 1], "req"
    )
    width = w_qkv.shape[2]
    heads_local = width // HD
    slots = k_cache.shape[1]
    full_rows = lax.all_gather(hidden_in, "mp", axis=1, tiled=True)
    normed = rms_scale(full_rows, attn_gain)
    blocks = normed.reshape(new_count, side, side, -1)
    columns = jnp.roll(blocks, (-row, -col), axis=(1, 2)).reshape(new_count, -1)
    projected = jnp.einsum(
        "nd,kdw->knw",
        columns,
        w_qkv_full,
        preferred_element_type=jnp.float32,
    )
    length = cache_len[0]
    positions = (length + jnp.arange(new_count, dtype=jnp.int32)).astype(jnp.float32)
    half = HD // 2
    lane = jnp.arange(width, dtype=jnp.int32)
    within = lane % HD
    partner_lane = lane - within + (within + half) % HD
    swap = (lane[:, None] == partner_lane[None, :]).astype(jnp.float32)
    partner = jnp.einsum(
        "knw,wv->knv", projected[:2], swap, precision=lax.Precision.HIGHEST,
        preferred_element_type=jnp.float32,
    )
    freq = THETA ** (-((within % half).astype(jnp.float32) * 2.0 / HD))
    angle = positions[:, None] * freq[None, :]
    cosine = jnp.cos(angle)
    sine = jnp.where(within < half, -1.0, 1.0)[None, :] * jnp.sin(angle)
    queries = (projected[0] * cosine + partner[0] * sine).astype(jnp.bfloat16).reshape(
        new_count, heads_local, HD
    )
    fresh_keys = (projected[1] * cosine + partner[1] * sine).astype(jnp.bfloat16).reshape(
        new_count, heads_local, HD
    )
    fresh_values = projected[2].astype(jnp.bfloat16).reshape(new_count, heads_local, HD)
    head_major = lambda array: array.reshape(array.shape[0], heads_local, HD).transpose(1, 0, 2)
    attn_heads = flash_attention(
        cache_len,
        queries.transpose(1, 0, 2),
        head_major(k_cache[0]),
        head_major(v_cache[0]),
        fresh_keys.transpose(1, 0, 2),
        fresh_values.transpose(1, 0, 2),
    )
    attn = attn_heads.transpose(1, 0, 2).reshape(new_count, width)
    partial_value = jnp.dot(
        attn, w_out_full, preferred_element_type=jnp.float32
    )
    summed = lax.psum(partial_value.astype(jnp.bfloat16), "mp").astype(jnp.float32)
    mid_full = (full_rows.astype(jnp.float32) + summed).astype(jnp.bfloat16)
    own = hidden_in.shape[1]
    mid_local = lax.dynamic_slice_in_dim(mid_full, lax.axis_index("mp") * own, own, axis=1)
    normed2 = rms_scale(mid_full, mlp_gain)
    columns = normed2
    gate = jnp.dot(
        columns,
        w_gate_full,
        preferred_element_type=jnp.float32,
    )
    upper = jnp.dot(
        columns, w_up_full, preferred_element_type=jnp.float32
    )
    units = (jax.nn.silu(gate) * upper).astype(jnp.bfloat16)
    terms = jnp.dot(
        units, w_down_full, preferred_element_type=jnp.float32
    )
    reduced = lax.psum_scatter(
        terms.astype(jnp.bfloat16), "mp", scatter_dimension=1, tiled=True
    ).astype(jnp.float32)
    hidden_out = (mid_local.astype(jnp.float32) + reduced).astype(jnp.bfloat16)
    return (
        hidden_out,
        fresh_keys.reshape(new_count, width),
        fresh_values.reshape(new_count, width),
    )


def solution(mesh):
    return jax.shard_map(
        on_device,
        mesh=mesh,
        in_specs=(
            P("req", "mp"),
            P(None, "req", "mp"),
            P("mp", "req"),
            P(),
            P(),
            P("req", "mp"),
            P("req", "mp"),
            P("mp", "req"),
            P("req", None, "mp"),
            P("req", None, "mp"),
            P("req"),
        ),
        out_specs=(P("req", "mp"), P("req", "mp"), P("req", "mp")),
        check_vma=False,
    )
```

profile of v0, /device:TPU:0, one launch (start us, length us, event | category | flops | bytes accessed | tf_op | source)
XLA Modules:
  0.0 329.8 jit_solution(8948437891027042417)
XLA Ops:
  7.2 0.0 all-gather.4.cloned.1.call-start
  7.2 0.7 all-gather.4.cloned.1.call-update
  7.9 0.0 all-gather.6.cloned.1.call-start
  8.0 1.1 reshape.139
  9.0 1.1 reshape.140
  10.1 2.0 pad_maximum_fusion
  12.1 0.0 all-gather.6.cloned.1.call-update
  12.1 0.0 all-reduce.2.cloned.1.call-start
  12.2 0.2 copy.69
  12.3 4.2 %collective-permute-start = (bf16[3,128,256]{1,2,0:T(8,128)(2,1)S(1)}, bf16[3,128,256]{1,2,0:T(8,128)(2,1)S(1)}, u32[]{:S(2)}, u32[]{:S(2)}) collective-permute-start(bf16[3,128,256]{1,2,0:T(8,128)(2,1)S(1)} %copy.69), channel_id=1, source_target_pairs={{0,24},{8,0},{16,8},{24,16},{32,56},{40,32},{48,40},{56,48},{64,88... | collective-permute-start | bytes 589832 | tf_op jit(solution)/shard_map/ppermute | solution.py:35
  16.5 0.0 collective-permute-start.1
  16.5 1.3 collective-permute-start.2
  18.4 3.0 copy.80
  21.4 3.2 copy.81
  24.6 2.9 copy.82
  27.5 3.2 copy.83
  30.8 0.0 collective-permute-done
  30.8 1.0 fusion.67
  31.8 3.0 collective-permute-start.3
  34.8 0.6 collective-permute-start.4
  35.4 1.0 collective-permute-start.5
  36.4 11.8 %all-gather.4.cloned.1.call-done = bf16[1024,2048]{1,0:T(8,128)(2,1)} async-done(((bf16[1024,256]{1,0:T(8,128)(2,1)}), bf16[1024,2048]{1,0:T(8,128)(2,1)}) %all-gather.4.cloned.1.call-update) | async-done | bytes 4194320 | tf_op jit(solution)/shard_map/all_gather | solution.py:162
  48.2 3.2 fusion.3
  51.5 0.2 copy-done
  51.7 3.1 fusion.5
  54.8 6.4 %copy.73 = bf16[1024,2048]{0,1:T(8,128)(2,1)} copy(bf16[1024,2048]{1,0:T(8,128)(2,1)} %fusion.5) | data formatting | bytes 8388608 | tf_op jit(solution)/shard_map/convert_element_type | solution.py:20
  61.1 6.4 %copy.74 = bf16[1024,4,4,128]{3,0,2,1:T(8,128)(2,1)} copy(bf16[1024,4,4,128]{0,3,2,1:T(8,128)(2,1)} %bitcast.63) | data formatting | bytes 8388608 | tf_op jit(solution)/shard_map/reshape | solution.py:164
  67.5 3.2 fusion.11
  70.7 6.4 %collective-permute-done.5 = bf16[3,4,128,256]{2,3,1,0:T(8,128)(2,1)} collective-permute-done((bf16[3,4,128,256]{2,3,1,0:T(8,128)(2,1)S(1)}, bf16[3,4,128,256]{2,3,1,0:T(8,128)(2,1)}, u32[]{:S(2)}, u32[]{:S(2)}) %collective-permute-start.5) | collective-permute-done | bytes 786464 | tf_op jit(solution)/shard_map/ppermute | solution.py:37
  77.1 5.2 %fusion.28 = f32[3,1024,256]{1,2,0:T(8,128)S(1)} fusion(s32[]{:T(128)S(6)} %select_n.97, bf16[1024,4,4,128]{3,0,2,1:T(8,128)(2,1)S(1)} %fusion.11, bf16[3,1,4,128,256]{3,4,2,0,1:T(8,128)(2,1)} %bitcast.7, bf16[3,1,4,128,256]{3,4,2,0,1:T(8,128)(2,1)} %bitcast.85, bf16[3,1,4,128,256]{3,4,2,0,1:T(8,128)(2,1)} %bitcast.84, ...), kind=kOutput, calls=%fused_computation.42 | convolution fusion | flops 3228041216 | bytes 10485764 | tf_op jit(solution)/shard_map/nd,kdw->knw/dot_general | solution.py:166
  82.3 0.9 slice.54
  83.1 1.3 fusion.46
  84.5 1.3 copy-done.1
  85.8 1.5 fusion.71
  87.3 3.2 copy.79
  90.5 3.2 copy.85
  93.7 1.5 fusion.70
  95.2 3.2 copy.77
  98.4 3.2 copy.84
  101.5 2.4 copy.86
  103.9 11.4 %fusion.43 = (bf16[4,1024,64]{2,1,0:T(8,128)(2,1)}, bf16[4,1024,64]{2,1,0:T(8,128)(2,1)}) fusion(f32[1024,4,64]{2,0,1:T(8,128)} %copy.85, f32[1024,4,64]{2,0,1:T(8,128)} %copy.84, f32[1024]{0:T(1024)S(1)} %add_convert_fusion.1, f32[4,64]{1,0:T(4,128)S(1)} %get-tuple-element.29, f32[4,64]{1,0:T(4,128)S(1)} %get-tuple-element.28, f32[1024,4,64]{2,0,1:T(8,128)} %copy.79, ...), kind=kLoop, calls=%fused_computation.51 | loop fusion | flops 2621440 | bytes 5249024 | tf_op jit(solution)/shard_map/transpose | solution.py:200
  115.3 37.3 %shard_map.130 = bf16[4,1024,64]{2,1,0:T(8,128)(2,1)} custom-call(s32[1]{0:T(128)} %copy.96.len_ref, bf16[4,1024,64]{2,1,0:T(8,128)(2,1)} %get-tuple-element.27.q_ref, bf16[4,4096,64]{2,1,0:T(8,128)(2,1)} %bitcast.69, bf16[4,4096,64]{2,1,0:T(8,128)(2,1)} %bitcast.70, bf16[4,1024,64]{2,1,0:T(8,128)(2,1)} %get-tuple-element.26.kn_ref, ...), custom_call_target="tpu_custom_call" | custom-call | flops 5368709120 | bytes 6815744 | tf_op jit(solution)/shard_map/pallas_call | solution.py:138
  152.6 2.3 copy.87
  154.9 2.3 slice_bitcast_fusion.1
  157.3 2.3 copy.88
  159.5 4.8 %convolution_convert_fusion = bf16[1024,2048]{1,0:T(8,128)(2,1)} fusion(bf16[1024,256]{0,1:T(8,128)(2,1)} %bitcast.76, bf16[256,2048]{0,1:T(8,128)(2,1)} %bitcast.68), kind=kOutput, calls=%fused_computation.22 | convolution fusion | flops 1075838976 | bytes 5767168 | tf_op jit(solution)/shard_map/dot_general | solution.py:204
  164.3 0.0 all-reduce.2.cloned.1.call-update
  164.3 0.0 reduce-scatter.2.cloned.1.call-start
  164.4 0.6 copy-done.7
  165.0 9.0 %fusion.69 = (bf16[16,1024,128]{2,1,0:T(8,128)(2,1)}, bf16[1024,16,128]{2,0,1:T(8,128)(2,1)}, bf16[16,1024,128]{2,1,0:T(8,128)(2,1)}) fusion(bf16[16,3328,128]{2,1,0:T(8,128)(2,1)} %bitcast.65), kind=kLoop, calls=%fused_computation.98 | loop fusion | bytes 25165824 | tf_op jit(solution)/shard_map/slice | solution.py:50
  174.0 7.3 %reshape_reshape.6 = bf16[2048,1024]{1,0:T(8,128)(2,1)} reshape(bf16[16,1024,128]{2,1,0:T(8,128)(2,1)} %get-tuple-element.19) | data formatting | bytes 8388608 | tf_op jit(solution)/shard_map/reshape;reshape | solution.py:54
  181.3 6.4 %copy.89 = bf16[1024,16,128]{0,2,1:T(8,128)(2,1)} copy(bf16[1024,16,128]{2,0,1:T(8,128)(2,1)} %get-tuple-element.18) | data formatting | bytes 8388608 | tf_op jit(solution)/shard_map/transpose | solution.py:51
  187.7 7.3 %reshape_reshape.7 = bf16[2048,1024]{1,0:T(8,128)(2,1)} reshape(bf16[16,1024,128]{2,1,0:T(8,128)(2,1)} %get-tuple-element.17) | data formatting | bytes 8388608 | tf_op jit(solution)/shard_map/reshape;reshape | solution.py:54
  195.1 60.7 %all-reduce.2.cloned.1.call-done = bf16[1024,2048]{1,0:T(8,128)(2,1)} async-done(((bf16[1024,2048]{1,0:T(8,128)(2,1)}), bf16[1024,2048]{1,0:T(8,128)(2,1)}) %all-reduce.2.cloned.1.call-update) | async-done | bytes 4194320 | tf_op jit(solution)/shard_map/psum | solution.py:207
  255.8 5.6 %fusion = (f32[1024]{0:T(1024)S(1)}, bf16[1024,2048]{1,0:T(8,128)(2,1)S(1)}) fusion(bf16[1024,2048]{1,0:T(8,128)(2,1)} %all-reduce.2.cloned.1.call-done, bf16[1024,2048]{1,0:T(8,128)(2,1)} %all-gather.4.cloned.1.call-done), kind=kLoop, calls=%fused_computation.5 | loop fusion | flops 14679040 | bytes 12587008 | tf_op jit(solution)/shard_map/reduce_sum | solution.py:19
  261.4 6.3 %fusion.34 = f32[1024,1024]{1,0:T(8,128)} fusion(bf16[2048,1024]{1,0:T(8,128)(2,1)S(1)} %copy-done.3, bf16[1024,2048]{1,0:T(8,128)(2,1)S(1)} %get-tuple-element.16, f32[2048]{0:T(1024)S(1)} %convert_element_type.95, f32[1024]{0:T(1024)S(1)} %add_rsqrt_fusion), kind=kOutput, calls=%fused_computation.45 | convolution fusion | flops 4303355904 | bytes 12595200 | tf_op jit(solution)/shard_map/dot_general | solution.py:213
  267.7 15.4 %convolution_convert_fusion.1 = bf16[1024,2048]{1,0:T(8,128)(2,1)} fusion(bf16[1024,2048]{0,1:T(8,128)(2,1)} %bitcast.71, f32[1024,1024]{1,0:T(8,128)} %fusion.34, bf16[2048,1024]{1,0:T(8,128)(2,1)} %reshape_reshape.7, bf16[1024,2048]{1,0:T(8,128)(2,1)} %copy-done.2, f32[2048]{0:T(1024)S(1)} %convert_element_type.95, f32[1024]{0:T(1024)S(1)} %add_rsqrt_fusion), kind=kOutput, calls=%fused_computation.23 | convolution fusion | flops 8606711808 | bytes 20983808 | tf_op jit(solution)/shard_map/dot_general | solution.py:222
  283.1 0.0 reduce-scatter.2.cloned.1.call-update
  283.1 5.8 %fusion.40 = bf16[1024,256]{0,1:T(8,128)(2,1)} fusion(f32[256]{0:T(256)S(1)} %get-tuple-element.30, f32[256]{0:T(256)S(1)} %get-tuple-element.31, f32[1024]{0:T(1024)S(1)} %add_convert_fusion.1, f32[2,1024,256]{1,2,0:T(8,128)} %copy-done.1, f32[3,1024,256]{1,2,0:T(8,128)S(1)} %fusion.28), kind=kLoop, calls=%fused_computation.48 | loop fusion | flops 1572864 | bytes 2627584 | tf_op jit(solution)/shard_map/convert_element_type | solution.py:190
  288.9 2.0 copy.90
  291.0 0.9 slice_bitcast_fusion.2
  291.8 2.1 copy.91
  293.9 27.3 %reduce-scatter.2.cloned.1.call-done = bf16[1024,256]{1,0:T(8,128)(2,1)} async-done(((bf16[1024,2048]{1,0:T(8,128)(2,1)}), bf16[1024,256]{1,0:T(8,128)(2,1)}) %reduce-scatter.2.cloned.1.call-update) | async-done | bytes 524304 | tf_op jit(solution)/shard_map/reduce_scatter | solution.py:225
  321.2 2.1 add_convert_fusion
  (30 shorter events, 0.1 us)
Async XLA Ops:
  7.2 5.0 %copy-start.5 = (bf16[3,128,256]{2,1,0:T(8,128)(2,1)S(1)}, bf16[3,128,256]{2,1,0:T(8,128)(2,1)}, u32[]{:S(2)}) copy-start(bf16[3,128,256]{2,1,0:T(8,128)(2,1)} %param.12) | copy-start | bytes 589828
  7.2 10.6 %copy-start.6 = (bf16[2048]{0:T(1024)(128)(2,1)S(1)}, bf16[2048]{0:T(1024)(128)(2,1)}, u32[]{:S(2)}) copy-start(bf16[2048]{0:T(1024)(128)(2,1)} %param.14) | copy-start | bytes 12292
  7.2 41.0 %all-gather.4.cloned.1.call-start = ((), (), s32[]{:S(2)}) async-start(), calls=%async_computation.1 | async-start | bytes 4718592 | tf_op jit(solution)/shard_map/all_gather | solution.py:162
  7.9 147.0 %all-gather.6.cloned.1.call-start = ((), (), s32[]{:S(2)}) async-start(), calls=%async_computation.4 | async-start | bytes 14483456 | tf_op jit(solution)/shard_map/all_gather | solution.py:45
  12.1 243.7 %all-reduce.2.cloned.1.call-start = ((), (), s32[]{:S(2)}) async-start(), calls=%async_computation.2 | async-start | bytes 8388608 | tf_op jit(solution)/shard_map/psum | solution.py:207
  12.3 18.4 %collective-permute-start = (bf16[3,128,256]{1,2,0:T(8,128)(2,1)S(1)}, bf16[3,128,256]{1,2,0:T(8,128)(2,1)S(1)}, u32[]{:S(2)}, u32[]{:S(2)}) collective-permute-start(bf16[3,128,256]{1,2,0:T(8,128)(2,1)S(1)} %copy.69), channel_id=1, source_target_pairs={{0,24},{8,0},{16,8},{24,16},{32,56},{40,32},{48,40},{56,48},{64,88... | collective-permute-start | bytes 589832 | tf_op jit(solution)/shard_map/ppermute | solution.py:35
  16.5 14.3 %collective-permute-start.1 = (bf16[3,128,256]{1,2,0:T(8,128)(2,1)S(1)}, bf16[3,128,256]{1,2,0:T(8,128)(2,1)S(1)}, u32[]{:S(2)}, u32[]{:S(2)}) collective-permute-start(bf16[3,128,256]{1,2,0:T(8,128)(2,1)S(1)} %copy.69), channel_id=1, source_target_pairs={{0,16},{8,24},{16,0},{24,8},{32,48},{40,56},{48,32},{56,40},{64,80... | collective-permute-start | bytes 589832 | tf_op jit(solution)/shard_map/ppermute | solution.py:35
  16.5 14.3 %collective-permute-start.2 = (bf16[3,128,256]{1,2,0:T(8,128)(2,1)S(1)}, bf16[3,128,256]{1,2,0:T(8,128)(2,1)S(1)}, u32[]{:S(2)}, u32[]{:S(2)}) collective-permute-start(bf16[3,128,256]{1,2,0:T(8,128)(2,1)S(1)} %copy.69), channel_id=1, source_target_pairs={{0,8},{8,16},{16,24},{24,0},{32,40},{40,48},{48,56},{56,32},{64,72... | collective-permute-start | bytes 589832 | tf_op jit(solution)/shard_map/ppermute | solution.py:35
  31.8 38.9 %collective-permute-start.3 = (bf16[3,4,128,256]{2,3,1,0:T(8,128)(2,1)S(1)}, bf16[3,4,128,256]{2,3,1,0:T(8,128)(2,1)S(1)}, u32[]{:S(2)}, u32[]{:S(2)}) collective-permute-start(bf16[3,4,128,256]{2,3,1,0:T(8,128)(2,1)S(1)} %get-tuple-element.25), channel_id=1, source_target_pairs={{0,96},{8,104},{16,112},{24,120},{32,0},{40,8},{48,16},{56,24},{64... | collective-permute-start | bytes 2359304 | tf_op jit(solution)/shard_map/ppermute | solution.py:37
  34.8 35.9 %collective-permute-start.4 = (bf16[3,4,128,256]{2,3,1,0:T(8,128)(2,1)S(1)}, bf16[3,4,128,256]{2,3,1,0:T(8,128)(2,1)S(1)}, u32[]{:S(2)}, u32[]{:S(2)}) collective-permute-start(bf16[3,4,128,256]{2,3,1,0:T(8,128)(2,1)S(1)} %get-tuple-element.25), channel_id=1, source_target_pairs={{0,64},{8,72},{16,80},{24,88},{32,96},{40,104},{48,112},{56,120},{... | collective-permute-start | bytes 2359304 | tf_op jit(solution)/shard_map/ppermute | solution.py:37
  35.4 41.7 %collective-permute-start.5 = (bf16[3,4,128,256]{2,3,1,0:T(8,128)(2,1)S(1)}, bf16[3,4,128,256]{2,3,1,0:T(8,128)(2,1)}, u32[]{:S(2)}, u32[]{:S(2)}) collective-permute-start(bf16[3,4,128,256]{2,3,1,0:T(8,128)(2,1)S(1)} %get-tuple-element.25), channel_id=1, source_target_pairs={{0,32},{8,40},{16,48},{24,56},{32,64},{40,72},{48,80},{56,88},{64,... | collective-permute-start | bytes 2359304 | tf_op jit(solution)/shard_map/ppermute | solution.py:37
  48.2 3.4 %copy-start = (bf16[1024,2048]{1,0:T(8,128)(2,1)S(1)}, bf16[1024,2048]{1,0:T(8,128)(2,1)}, u32[]{:S(2)}) copy-start(bf16[1024,2048]{1,0:T(8,128)(2,1)} %all-gather.4.cloned.1.call-done) | copy-start | bytes 12582916
  67.5 9.6 %copy-start.4 = (bf16[3,1,4,128,256]{3,4,2,0,1:T(8,128)(2,1)S(1)}, bf16[3,1,4,128,256]{3,4,2,0,1:T(8,128)(2,1)}, u32[]{:S(2)}) copy-start(bf16[3,1,4,128,256]{3,4,2,0,1:T(8,128)(2,1)} %get-tuple-element.24) | copy-start | bytes 2359300
  70.7 6.4 %copy-start.8 = (bf16[3,4,128,256]{2,3,1,0:T(8,128)(2,1)}, bf16[3,4,128,256]{2,3,1,0:T(8,128)(2,1)S(1)}, u32[]{:S(2)}) copy-start(bf16[3,4,128,256]{2,3,1,0:T(8,128)(2,1)S(1)} %collective-permute-done.3) | copy-start | bytes 2359300
  70.7 6.4 %copy-start.9 = (bf16[3,4,128,256]{2,3,1,0:T(8,128)(2,1)}, bf16[3,4,128,256]{2,3,1,0:T(8,128)(2,1)S(1)}, u32[]{:S(2)}) copy-start(bf16[3,4,128,256]{2,3,1,0:T(8,128)(2,1)S(1)} %collective-permute-done.4) | copy-start | bytes 2359300
  84.5 1.3 copy-start.1
  164.3 0.7 copy-start.7
  164.3 156.9 %reduce-scatter.2.cloned.1.call-start = ((), (), s32[]{:S(2)}) async-start(), calls=%async_computation.3 | async-start | bytes 4718592 | tf_op jit(solution)/shard_map/reduce_scatter | solution.py:225
  255.8 5.6 %copy-start.3 = (bf16[2048,1024]{1,0:T(8,128)(2,1)S(1)}, bf16[2048,1024]{1,0:T(8,128)(2,1)}, u32[]{:S(2)}) copy-start(bf16[2048,1024]{1,0:T(8,128)(2,1)} %reshape_reshape.6) | copy-start | bytes 12582916
  261.4 6.4 %copy-start.2 = (bf16[1024,2048]{1,0:T(8,128)(2,1)}, bf16[1024,2048]{1,0:T(8,128)(2,1)S(1)}, u32[]{:S(2)}) copy-start(bf16[1024,2048]{1,0:T(8,128)(2,1)S(1)} %get-tuple-element.16) | copy-start | bytes 12582916
Sparse Core Ops, SparseCore 0:
  9.7 38.4 all-gather.3
  50.4 100.5 all-gather.5
  164.4 91.2 all-reduce.1
  283.2 37.9 reduce-scatter.1
where the time goes:
time: 333 us; the launch traced here: 330 us
  waiting for transfers between devices  107 us (32%)
  local copies, waits for them, and re-layouts  90.4 us (27%)
  other arithmetic  37.4 us (11%)
  Pallas kernels  37.3 us (11%)
  matrix products  32.9 us (10%)
  between operations  14.6 us (4%)
  starting transfers between devices  10.2 us (3%)
    psum x1, waiting for transfers between devices, on_device(): lax.psum(partial_value.astype(jnp.bfloat16), 'mp').astype(jnp.float32)  60.7 us
    pallas_call x1, Pallas kernels, flash_attention(): pl.pallas_call(body, grid_spec=grid_spec, out_shape=jax.ShapeDtypeStruct(...  37.3 us
    reduce_scatter x1, waiting for transfers between devices, on_device(): lax.psum_scatter(terms.astype(jnp.bfloat16), 'mp', scatter_dimension=1, t...  27.3 us
    dot_general x1, matrix products, on_device(): terms = jnp.dot(units, w_down_full, preferred_element_type=jnp.float32)  15.4 us
    another operation x2, local copies, waits for them, and re-layouts, gather_packed(): outs.append(piece.reshape(shape))  14.7 us
    unnamed x25, local copies, waits for them, and re-layouts  12.3 us
    all_gather x1, waiting for transfers between devices, on_device(): full_rows = lax.all_gather(hidden_in, 'mp', axis=1, tiled=True)  11.8 us
    transpose x1, other arithmetic, on_device(): fresh_keys.transpose(1, 0, 2)  11.4 us
  transfers between devices with their start and end apart: 10, of which 4 were waited for; matrix products, arithmetic and copies ran while one was open for 36% of the time, Pallas kernels for 11%

commit v1 on v0

--- a/solution.py
+++ b/solution.py
@@ -59,7 +59,8 @@
 def flash_body(len_ref, q_ref, kc_ref, vc_ref, kn_ref, vn_ref, o_ref, m_sc, l_sc, acc_sc, *, tk, n_cache, scale):
     j = pl.program_id(1)
     length = len_ref[0]
-    tq = q_ref.shape[1]
+    tq = q_ref.shape[0]
+    pair = q_ref.shape[1] // HD
 
     @pl.when(j == 0)
     def _():
@@ -67,78 +68,86 @@
         l_sc[...] = jnp.zeros(l_sc.shape, jnp.float32)
         acc_sc[...] = jnp.zeros(acc_sc.shape, jnp.float32)
 
-    def update(k, v, mask):
-        s = lax.dot_general(q_ref[0] * scale, k, (((1,), (1,)), ((), ())), preferred_element_type=jnp.float32)
-        if mask is not None:
-            s = jnp.where(mask, s, NEG_FILL)
-        m_prev = m_sc[...]
-        m_new = jnp.maximum(m_prev, jnp.max(s, axis=1, keepdims=True))
-        alpha = jnp.exp(m_prev - m_new)
-        p = jnp.exp(s - m_new)
-        if mask is not None:
-            p = jnp.where(mask, p, 0.0)
-        l_sc[...] = alpha * l_sc[...] + jnp.sum(p, axis=1, keepdims=True)
-        acc_sc[...] = alpha * acc_sc[...] + jnp.dot(p.astype(jnp.bfloat16), v, preferred_element_type=jnp.float32)
-        m_sc[...] = m_new
+    def update(k_ref, v_ref, mask):
+        for head in range(pair):
+            lanes = pl.ds(head * HD, HD)
+            q = q_ref[:, lanes] * scale
+            s = lax.dot_general(q, k_ref[:, lanes], (((1,), (1,)), ((), ())), preferred_element_type=jnp.float32)
+            if mask is not None:
+                s = jnp.where(mask, s, NEG_FILL)
+            m_prev = m_sc[head]
+            m_new = jnp.maximum(m_prev, jnp.max(s, axis=1, keepdims=True))
+            alpha = jnp.exp(m_prev - m_new)
+            p = jnp.exp(s - m_new)
+            if mask is not None:
+                p = jnp.where(mask, p, 0.0)
+            l_sc[head] = alpha * l_sc[head] + jnp.sum(p, axis=1, keepdims=True)
+            acc_sc[head] = alpha * acc_sc[head] + jnp.dot(
+                p.astype(jnp.bfloat16), v_ref[:, lanes], preferred_element_type=jnp.float32
+            )
+            m_sc[head] = m_new
 
     begin = j * tk
 
     @pl.when((j < n_cache) & (begin + tk <= length))
     def _():
-        update(kc_ref[0], vc_ref[0], None)
+        update(kc_ref, vc_ref, None)
 
     @pl.when((j < n_cache) & (begin < length) & (begin + tk > length))
     def _():
         col = begin + lax.broadcasted_iota(jnp.int32, (tq, tk), 1)
-        update(kc_ref[0], vc_ref[0], col < length)
+        update(kc_ref, vc_ref, col < length)
 
     @pl.when(j == n_cache)
     def _():
         row = lax.broadcasted_iota(jnp.int32, (tq, tq), 0)
         col = lax.broadcasted_iota(jnp.int32, (tq, tq), 1)
-        update(kn_ref[0], vn_ref[0], row >= col)
-        o_ref[0] = (acc_sc[...] / l_sc[...]).astype(o_ref.dtype)
+        update(kn_ref, vn_ref, row >= col)
+        for head in range(pair):
+            o_ref[:, pl.ds(head * HD, HD)] = (acc_sc[head] / l_sc[head]).astype(o_ref.dtype)
 
 
 def flash_attention(length, q, kc, vc, kn, vn):
-    heads, new_count, hd = q.shape
-    slots = kc.shape[1]
+    new_count, width = q.shape
+    slots = kc.shape[0]
     tk = min(new_count, slots)
     n_cache = slots // tk
-    body = functools.partial(flash_body, tk=tk, n_cache=n_cache, scale=hd ** (-0.5))
+    lanes = 2 * HD if width % (2 * HD) == 0 else width
+    pair = lanes // HD
+    body = functools.partial(flash_body, tk=tk, n_cache=n_cache, scale=HD ** (-0.5))
 
     def cache_map(h, j, len_ref):
         last = jnp.maximum(len_ref[0] - 1, 0) // tk
-        return (h, jnp.minimum(j, last), 0)
-
-    fixed = lambda h, j, len_ref: (h, 0, 0)
+        return (jnp.minimum(j, last), h)
+
+    fixed = lambda h, j, len_ref: (0, h)
     grid_spec = pltpu.PrefetchScalarGridSpec(
         num_scalar_prefetch=1,
-        grid=(heads, n_cache + 1),
+        grid=(width // lanes, n_cache + 1),
         in_specs=[
-            pl.BlockSpec((1, new_count, hd), fixed),
-            pl.BlockSpec((1, tk, hd), cache_map),
-            pl.BlockSpec((1, tk, hd), cache_map),
-            pl.BlockSpec((1, new_count, hd), fixed),
-            pl.BlockSpec((1, new_count, hd), fixed),
+            pl.BlockSpec((new_count, lanes), fixed),
+            pl.BlockSpec((tk, lanes), cache_map),
+            pl.BlockSpec((tk, lanes), cache_map),
+            pl.BlockSpec((new_count, lanes), fixed),
+            pl.BlockSpec((new_count, lanes), fixed),
         ],
-        out_specs=pl.BlockSpec((1, new_count, hd), fixed),
+        out_specs=pl.BlockSpec((new_count, lanes), fixed),
         scratch_shapes=[
-            pltpu.VMEM((new_count, 1), jnp.float32),
-            pltpu.VMEM((new_count, 1), jnp.float32),
-            pltpu.VMEM((new_count, hd), jnp.float32),
+            pltpu.VMEM((pair, new_count, 1), jnp.float32),
+            pltpu.VMEM((pair, new_count, 1), jnp.float32),
+            pltpu.VMEM((pair, new_count, HD), jnp.float32),
         ],
     )
-    flops = 4 * heads * new_count * (slots + new_count) * hd
+    heads = width // HD
     cost = pl.CostEstimate(
-        flops=flops,
+        flops=4 * heads * new_count * (slots + new_count) * HD,
         transcendentals=heads * new_count * (slots + new_count),
-        bytes_accessed=2 * (q.size + kc.size + vc.size + kn.size + vn.size) + 4 * q.size,
+        bytes_accessed=2 * (q.size + kc.size + vc.size + kn.size + vn.size) + 2 * q.size,
     )
     return pl.pallas_call(
         body,
         grid_spec=grid_spec,
-        out_shape=jax.ShapeDtypeStruct((heads, new_count, hd), jnp.bfloat16),
+        out_shape=jax.ShapeDtypeStruct((new_count, width), jnp.bfloat16),
         compiler_params=pltpu.CompilerParams(
             dimension_semantics=("arbitrary", "arbitrary"), vmem_limit_bytes=56 * 1024 * 1024
         ),
@@ -191,16 +200,14 @@
         new_count, heads_local, HD
     )
     fresh_values = projected[2].astype(jnp.bfloat16).reshape(new_count, heads_local, HD)
-    head_major = lambda array: array.reshape(array.shape[0], heads_local, HD).transpose(1, 0, 2)
-    attn_heads = flash_attention(
+    attn = flash_attention(
         cache_len,
-        queries.transpose(1, 0, 2),
-        head_major(k_cache[0]),
-        head_major(v_cache[0]),
-        fresh_keys.transpose(1, 0, 2),
-        fresh_values.transpose(1, 0, 2),
-    )
-    attn = attn_heads.transpose(1, 0, 2).reshape(new_count, width)
+        queries.reshape(new_count, width),
+        k_cache[0],
+        v_cache[0],
+        fresh_keys.reshape(new_count, width),
+        fresh_values.reshape(new_count, width),
+    )
     partial_value = jnp.dot(
         attn, w_out_full, preferred_element_type=jnp.float32
     )

time: 333 us -> 300 us (0.901)
  local copies, waits for them, and re-layouts: 90.4 us -> 49 us
  waiting for transfers between devices: 107 us -> 127 us
  other arithmetic: 37.4 us -> 24.8 us
  Pallas kernels: 37.3 us -> 41.9 us
    all_gather x1, waiting for transfers between devices: 0.01 us -> 20.1 us  [gather_packed(): gathered = lax.all_gather(joined, axis_name, axis=0, tiled=False)]
    psum x1, waiting for transfers between devices: 60.7 us -> 41.3 us  [on_device(): lax.psum(partial_value.astype(jnp.bfloat16), 'mp').astype(jnp.float32)]
    squeeze x4 -> x0, local copies, waits for them, and re-layouts: 12.7 us -> none  [the longest x1 3.23 us: on_device(): partner[1] * sine]
    transpose x1 -> x0, other arithmetic: 11.4 us -> none  [on_device(): fresh_keys.transpose(1, 0, 2)]
    unnamed x25 -> x15, local copies, waits for them, and re-layouts: 12.3 us -> 1.01 us
    reduce_scatter x1, waiting for transfers between devices: 27.3 us -> 38 us  [on_device(): lax.psum_scatter(terms.astype(jnp.bfloat16), 'mp', scatter_dimension=1, t...]
    ppermute x3, waiting for transfers between devices: 0.01 us -> 9.82 us  [gather_req_shifted(): lax.ppermute(block, axis_name, inner(k))]
    another operation x2 -> x0, local copies, waits for them, and re-layouts: 6.39 us -> none  [on_device(): array.reshape(array.shape[0], heads_local, HD).transpose(1, 0, 2)]
  transfers between devices with their start and end apart: 10 -> 10, of which waited for: 4 -> 8; matrix products, arithmetic and copies ran while one was open for 36% -> 23% of each run, Pallas kernels for 11% -> 14%
where the time goes in v1:
time: 300 us; the launch traced here: 299 us
  waiting for transfers between devices  127 us (42%)
  local copies, waits for them, and re-layouts  49 us (16%)
  Pallas kernels  41.9 us (14%)
  matrix products  31.6 us (11%)
  other arithmetic  24.8 us (8%)
  between operations  14.6 us (5%)
  starting transfers between devices  10.3 us (3%)
    pallas_call x1, Pallas kernels, flash_attention(): pl.pallas_call(body, grid_spec=grid_spec, out_shape=jax.ShapeDtypeStruct(...  41.9 us
    psum x1, waiting for transfers between devices, on_device(): lax.psum(partial_value.astype(jnp.bfloat16), 'mp').astype(jnp.float32)  41.3 us
    reduce_scatter x1, waiting for transfers between devices, on_device(): lax.psum_scatter(terms.astype(jnp.bfloat16), 'mp', scatter_dimension=1, t...  38 us
    all_gather x1, waiting for transfers between devices, gather_packed(): gathered = lax.all_gather(joined, axis_name, axis=0, tiled=False)  20.1 us
    dot_general x1, matrix products, on_device(): terms = jnp.dot(units, w_down_full, preferred_element_type=jnp.float32)  15.4 us
    all_gather x1, waiting for transfers between devices, on_device(): full_rows = lax.all_gather(hidden_in, 'mp', axis=1, tiled=True)  15.1 us
    another operation x2, local copies, waits for them, and re-layouts, gather_packed(): outs.append(piece.reshape(shape))  14.8 us
    ppermute x3, waiting for transfers between devices, gather_req_shifted(): lax.ppermute(block, axis_name, inner(k))  9.82 us
  transfers between devices with their start and end apart: 10, of which 8 were waited for; matrix products, arithmetic and copies ran while one was open for 23% of the time, Pallas kernels for 14%

profile of v1, /device:TPU:0, one launch (start us, length us, event | category | flops | bytes accessed | tf_op | source)
XLA Modules:
  0.0 298.7 jit_solution(17285781406137259796)
XLA Ops:
  7.2 0.0 copy-start.4
  7.2 0.0 copy-start.5
  7.2 0.0 all-gather.4.cloned.1.call-start
  7.2 0.7 all-gather.4.cloned.1.call-update
  7.9 0.0 all-gather.6.cloned.1.call-start
  8.0 1.1 reshape.94
  9.0 1.1 reshape.95
  10.1 2.0 pad_maximum_fusion
  12.1 0.0 all-gather.6.cloned.1.call-update
  12.1 0.0 all-reduce.2.cloned.1.call-start
  12.1 0.0 copy-done.4
  12.1 0.2 copy.33
  12.3 4.2 %collective-permute-start = (bf16[3,128,256]{1,2,0:T(8,128)(2,1)S(1)}, bf16[3,128,256]{1,2,0:T(8,128)(2,1)S(1)}, u32[]{:S(2)}, u32[]{:S(2)}) collective-permute-start(bf16[3,128,256]{1,2,0:T(8,128)(2,1)S(1)} %copy.33), channel_id=1, source_target_pairs={{0,24},{8,0},{16,8},{24,16},{32,56},{40,32},{48,40},{56,48},{64,88... | collective-permute-start | bytes 589832 | tf_op jit(solution)/shard_map/ppermute | solution.py:35
  16.5 0.0 collective-permute-start.1
  16.5 1.3 collective-permute-start.2
  17.8 0.0 copy-done.5
  18.5 6.4 %collective-permute-done = bf16[3,128,256]{1,2,0:T(8,128)(2,1)S(1)} collective-permute-done((bf16[3,128,256]{1,2,0:T(8,128)(2,1)S(1)}, bf16[3,128,256]{1,2,0:T(8,128)(2,1)S(1)}, u32[]{:S(2)}, u32[]{:S(2)}) %collective-permute-start) | collective-permute-done | bytes 196640 | tf_op jit(solution)/shard_map/ppermute | solution.py:35
  24.9 1.0 collective-permute-done.1
  25.8 2.5 collective-permute-done.2
  28.3 0.1 fusion.53
  28.4 3.1 %collective-permute-start.3 = (bf16[3,4,128,256]{2,3,1,0:T(8,128)(2,1)S(1)}, bf16[3,4,128,256]{2,3,1,0:T(8,128)(2,1)S(1)}, u32[]{:S(2)}, u32[]{:S(2)}) collective-permute-start(bf16[3,4,128,256]{2,3,1,0:T(8,128)(2,1)S(1)} %get-tuple-element.11), channel_id=1, source_target_pairs={{0,96},{8,104},{16,112},{24,120},{32,0},{40,8},{48,16},{56,24},{64... | collective-permute-start | bytes 2359304 | tf_op jit(solution)/shard_map/ppermute | solution.py:37
  31.5 0.6 collective-permute-start.4
  32.1 1.0 collective-permute-start.5
  33.1 15.1 %all-gather.4.cloned.1.call-done = bf16[1024,2048]{1,0:T(8,128)(2,1)} async-done(((bf16[1024,256]{1,0:T(8,128)(2,1)}), bf16[1024,2048]{1,0:T(8,128)(2,1)}) %all-gather.4.cloned.1.call-update) | async-done | bytes 4194320 | tf_op jit(solution)/shard_map/all_gather | solution.py:171
  48.2 0.0 copy-start
  48.2 3.2 %fusion.3 = f32[1024]{0:T(1024)S(1)} fusion(bf16[1024,2048]{1,0:T(8,128)(2,1)} %all-gather.4.cloned.1.call-done), kind=kLoop, calls=%fused_computation.8 | loop fusion | flops 6290432 | bytes 4198400 | tf_op jit(solution)/shard_map/reduce_sum | solution.py:19
  51.5 0.2 copy-done
  51.7 3.0 %fusion.5 = bf16[1024,2048]{1,0:T(8,128)(2,1)} fusion(bf16[1024,2048]{1,0:T(8,128)(2,1)S(1)} %copy-done, f32[2048]{0:T(1024)S(1)} %convert_element_type.68, f32[1024]{0:T(1024)S(1)} %add_rsqrt_fusion.1), kind=kLoop, calls=%fused_computation.10 | loop fusion | flops 8388608 | bytes 8400896 | tf_op jit(solution)/shard_map/convert_element_type | solution.py:20
  54.7 6.4 %copy.37 = bf16[1024,2048]{0,1:T(8,128)(2,1)} copy(bf16[1024,2048]{1,0:T(8,128)(2,1)} %fusion.5) | data formatting | bytes 8388608 | tf_op jit(solution)/shard_map/convert_element_type | solution.py:20
  61.1 6.4 %copy.38 = bf16[1024,4,4,128]{3,0,2,1:T(8,128)(2,1)} copy(bf16[1024,4,4,128]{0,3,2,1:T(8,128)(2,1)} %bitcast.59) | data formatting | bytes 8388608 | tf_op jit(solution)/shard_map/reshape | solution.py:173
  67.5 3.1 %fusion.11 = bf16[1024,4,4,128]{3,0,2,1:T(8,128)(2,1)S(1)} fusion(s32[]{:T(128)S(6)} %select_n.82, bf16[1024,4,4,128]{3,0,2,1:T(8,128)(2,1)} %copy.38), kind=kLoop, calls=%fused_computation.19 | loop fusion | flops 2097152 | bytes 8388612 | tf_op jit(solution)/shard_map/jit(_roll_dynamic)/concatenate | solution.py:174
  70.6 0.0 collective-permute-done.3
  70.6 0.0 collective-permute-done.4
  70.7 1.4 collective-permute-done.5
  72.1 5.4 %fusion.19 = f32[3,1024,256]{2,1,0:T(8,128)S(1)} fusion(s32[]{:T(128)S(6)} %select_n.85, bf16[1024,4,4,128]{3,0,2,1:T(8,128)(2,1)S(1)} %fusion.11, bf16[3,1,4,128,256]{3,4,2,0,1:T(8,128)(2,1)} %bitcast.7, bf16[3,1,4,128,256]{3,4,2,0,1:T(8,128)(2,1)} %bitcast.6, bf16[3,1,4,128,256]{3,4,2,0,1:T(8,128)(2,1)S(1)} %bitcast.70, ...), kind=kOutput, calls=%fused_computation.31 | convolution fusion | flops 3228041216 | bytes 10485764 | tf_op jit(solution)/shard_map/nd,kdw->knw/dot_general | solution.py:175
  77.5 0.8 fusion.38.vn_ref
  78.4 1.2 fusion.40
  79.5 5.6 %fusion.34 = (bf16[1024,256]{1,0:T(8,128)(2,1)}, bf16[1024,256]{1,0:T(8,128)(2,1)}) fusion(f32[2,1024,256]{2,1,0:T(8,128)S(1)} %fusion.40, f32[3,1024,256]{2,1,0:T(8,128)S(1)} %fusion.19, f32[256]{0:T(256)S(1)} %get-tuple-element.12, f32[256]{0:T(256)S(1)} %get-tuple-element.13, f32[1024]{0:T(1024)S(1)} %add_convert_fusion.1), kind=kLoop, calls=%fused_computation.40 | loop fusion | flops 2621440 | bytes 5249024 | tf_op jit(solution)/shard_map/convert_element_type | solution.py:199
  85.1 41.9 %shard_map.130 = bf16[1024,256]{1,0:T(8,128)(2,1)} custom-call(s32[1]{0:T(128)} %copy.47.len_ref, bf16[1024,256]{1,0:T(8,128)(2,1)} %get-tuple-element.9.q_ref, bf16[4096,256]{1,0:T(8,128)(2,1)} %bitcast.68, bf16[4096,256]{1,0:T(8,128)(2,1)} %bitcast.69, bf16[1024,256]{1,0:T(8,128)(2,1)} %get-tuple-element.8.kn_ref, bf16[1024,256]{1,0:T(8,128)(2,1)} %fusion.38.vn_ref), custom_call_target="tpu_custom_call" | custom-call | flops 5368709120 | bytes 6291456 | tf_op jit(solution)/shard_map/pallas_call | solution.py:147
  127.0 0.0 copy-start.3
  127.0 20.1 %all-gather.6.cloned.1.call-done = bf16[53248,128]{1,0:T(8,128)(2,1)} async-done(((bf16[3328,128]{1,0:T(8,128)(2,1)}), bf16[53248,128]{1,0:T(8,128)(2,1)}) %all-gather.6.cloned.1.call-update) | async-done | bytes 13631504 | tf_op jit(solution)/shard_map/all_gather | solution.py:45
  147.1 1.3 slice_bitcast_fusion.1
  148.4 0.5 copy.41
  149.0 0.0 copy-done.3
  149.0 3.3 %convolution_convert_fusion = bf16[1024,2048]{1,0:T(8,128)(2,1)} fusion(bf16[1024,256]{1,0:T(8,128)(2,1)S(1)} %copy-done.3, bf16[256,2048]{0,1:T(8,128)(2,1)S(1)} %bitcast.62), kind=kOutput, calls=%fused_computation.22 | convolution fusion | flops 1075838976 | bytes 5767168 | tf_op jit(solution)/shard_map/dot_general | solution.py:211
  152.3 0.0 copy-start.6
  152.3 0.0 all-reduce.2.cloned.1.call-update
  152.3 0.0 reduce-scatter.2.cloned.1.call-start
  152.3 0.6 copy-done.6
  153.0 9.1 %fusion.55 = (bf16[16,1024,128]{2,1,0:T(8,128)(2,1)}, bf16[1024,16,128]{2,0,1:T(8,128)(2,1)}, bf16[16,1024,128]{2,1,0:T(8,128)(2,1)}) fusion(bf16[16,3328,128]{2,1,0:T(8,128)(2,1)} %bitcast.61), kind=kLoop, calls=%fused_computation.80 | loop fusion | bytes 25165824 | tf_op jit(solution)/shard_map/slice | solution.py:50
  162.1 7.4 %reshape_reshape.6 = bf16[2048,1024]{1,0:T(8,128)(2,1)} reshape(bf16[16,1024,128]{2,1,0:T(8,128)(2,1)} %get-tuple-element.7) | data formatting | bytes 8388608 | tf_op jit(solution)/shard_map/reshape;reshape | solution.py:54
  169.5 6.4 %copy.42 = bf16[1024,16,128]{0,2,1:T(8,128)(2,1)} copy(bf16[1024,16,128]{2,0,1:T(8,128)(2,1)} %get-tuple-element.6) | data formatting | bytes 8388608 | tf_op jit(solution)/shard_map/transpose | solution.py:51
  175.9 7.4 %reshape_reshape.7 = bf16[2048,1024]{1,0:T(8,128)(2,1)} reshape(bf16[16,1024,128]{2,1,0:T(8,128)(2,1)} %get-tuple-element.5) | data formatting | bytes 8388608 | tf_op jit(solution)/shard_map/reshape;reshape | solution.py:54
  183.3 41.3 %all-reduce.2.cloned.1.call-done = bf16[1024,2048]{1,0:T(8,128)(2,1)} async-done(((bf16[1024,2048]{1,0:T(8,128)(2,1)}), bf16[1024,2048]{1,0:T(8,128)(2,1)}) %all-reduce.2.cloned.1.call-update) | async-done | bytes 4194320 | tf_op jit(solution)/shard_map/psum | solution.py:214
  224.6 0.0 copy-start.2
  224.6 5.6 %fusion = (f32[1024]{0:T(1024)S(1)}, bf16[1024,2048]{1,0:T(8,128)(2,1)S(1)}) fusion(bf16[1024,2048]{1,0:T(8,128)(2,1)} %all-reduce.2.cloned.1.call-done, bf16[1024,2048]{1,0:T(8,128)(2,1)} %all-gather.4.cloned.1.call-done), kind=kLoop, calls=%fused_computation.5 | loop fusion | flops 14679040 | bytes 12587008 | tf_op jit(solution)/shard_map/reduce_sum | solution.py:19
  230.2 0.0 copy-start.1
  230.2 0.0 copy-done.2
  230.3 6.3 %fusion.27 = f32[1024,1024]{1,0:T(8,128)} fusion(bf16[2048,1024]{1,0:T(8,128)(2,1)S(1)} %copy-done.2, bf16[1024,2048]{1,0:T(8,128)(2,1)S(1)} %get-tuple-element.4, f32[2048]{0:T(1024)S(1)} %convert_element_type.80, f32[1024]{0:T(1024)S(1)} %add_rsqrt_fusion), kind=kOutput, calls=%fused_computation.36 | convolution fusion | flops 4303355904 | bytes 12595200 | tf_op jit(solution)/shard_map/dot_general | solution.py:220
  236.6 0.0 copy-done.1
  236.6 15.4 %convolution_convert_fusion.1 = bf16[1024,2048]{1,0:T(8,128)(2,1)} fusion(bf16[1024,2048]{0,1:T(8,128)(2,1)} %bitcast.63, f32[1024,1024]{1,0:T(8,128)} %fusion.27, bf16[2048,1024]{1,0:T(8,128)(2,1)} %reshape_reshape.7, bf16[1024,2048]{1,0:T(8,128)(2,1)} %copy-done.1, f32[2048]{0:T(1024)S(1)} %convert_element_type.80, f32[1024]{0:T(1024)S(1)} %add_rsqrt_fusion), kind=kOutput, calls=%fused_computation.23 | convolution fusion | flops 8606711808 | bytes 20983808 | tf_op jit(solution)/shard_map/dot_general | solution.py:229
  252.0 0.0 reduce-scatter.2.cloned.1.call-update
  252.0 38.0 %reduce-scatter.2.cloned.1.call-done = bf16[1024,256]{1,0:T(8,128)(2,1)} async-done(((bf16[1024,2048]{1,0:T(8,128)(2,1)}), bf16[1024,256]{1,0:T(8,128)(2,1)}) %reduce-scatter.2.cloned.1.call-update) | async-done | bytes 524304 | tf_op jit(solution)/shard_map/reduce_scatter | solution.py:232
  290.0 2.1 add_convert_fusion
  (7 shorter events, 0.0 us)
Async XLA Ops:
  7.2 5.0 %copy-start.4 = (bf16[3,128,256]{2,1,0:T(8,128)(2,1)S(1)}, bf16[3,128,256]{2,1,0:T(8,128)(2,1)}, u32[]{:S(2)}) copy-start(bf16[3,128,256]{2,1,0:T(8,128)(2,1)} %param.12) | copy-start | bytes 589828
  7.2 10.6 %copy-start.5 = (bf16[2048]{0:T(1024)(128)(2,1)S(1)}, bf16[2048]{0:T(1024)(128)(2,1)}, u32[]{:S(2)}) copy-start(bf16[2048]{0:T(1024)(128)(2,1)} %param.14) | copy-start | bytes 12292
  7.2 41.0 %all-gather.4.cloned.1.call-start = ((), (), s32[]{:S(2)}) async-start(), calls=%async_computation.1 | async-start | bytes 4718592 | tf_op jit(solution)/shard_map/all_gather | solution.py:171
  7.9 139.2 %all-gather.6.cloned.1.call-start = ((), (), s32[]{:S(2)}) async-start(), calls=%async_computation.4 | async-start | bytes 14483456 | tf_op jit(solution)/shard_map/all_gather | solution.py:45
  12.1 212.5 %all-reduce.2.cloned.1.call-start = ((), (), s32[]{:S(2)}) async-start(), calls=%async_computation.2 | async-start | bytes 8388608 | tf_op jit(solution)/shard_map/psum | solution.py:214
  12.3 12.6 %collective-permute-start = (bf16[3,128,256]{1,2,0:T(8,128)(2,1)S(1)}, bf16[3,128,256]{1,2,0:T(8,128)(2,1)S(1)}, u32[]{:S(2)}, u32[]{:S(2)}) collective-permute-start(bf16[3,128,256]{1,2,0:T(8,128)(2,1)S(1)} %copy.33), channel_id=1, source_target_pairs={{0,24},{8,0},{16,8},{24,16},{32,56},{40,32},{48,40},{56,48},{64,88... | collective-permute-start | bytes 589832 | tf_op jit(solution)/shard_map/ppermute | solution.py:35
  16.5 9.3 %collective-permute-start.1 = (bf16[3,128,256]{1,2,0:T(8,128)(2,1)S(1)}, bf16[3,128,256]{1,2,0:T(8,128)(2,1)S(1)}, u32[]{:S(2)}, u32[]{:S(2)}) collective-permute-start(bf16[3,128,256]{1,2,0:T(8,128)(2,1)S(1)} %copy.33), channel_id=1, source_target_pairs={{0,16},{8,24},{16,0},{24,8},{32,48},{40,56},{48,32},{56,40},{64,80... | collective-permute-start | bytes 589832 | tf_op jit(solution)/shard_map/ppermute | solution.py:35
  16.5 11.8 %collective-permute-start.2 = (bf16[3,128,256]{1,2,0:T(8,128)(2,1)S(1)}, bf16[3,128,256]{1,2,0:T(8,128)(2,1)S(1)}, u32[]{:S(2)}, u32[]{:S(2)}) collective-permute-start(bf16[3,128,256]{1,2,0:T(8,128)(2,1)S(1)} %copy.33), channel_id=1, source_target_pairs={{0,8},{8,16},{16,24},{24,0},{32,40},{40,48},{48,56},{56,32},{64,72... | collective-permute-start | bytes 589832 | tf_op jit(solution)/shard_map/ppermute | solution.py:35
  28.4 42.2 %collective-permute-start.3 = (bf16[3,4,128,256]{2,3,1,0:T(8,128)(2,1)S(1)}, bf16[3,4,128,256]{2,3,1,0:T(8,128)(2,1)S(1)}, u32[]{:S(2)}, u32[]{:S(2)}) collective-permute-start(bf16[3,4,128,256]{2,3,1,0:T(8,128)(2,1)S(1)} %get-tuple-element.11), channel_id=1, source_target_pairs={{0,96},{8,104},{16,112},{24,120},{32,0},{40,8},{48,16},{56,24},{64... | collective-permute-start | bytes 2359304 | tf_op jit(solution)/shard_map/ppermute | solution.py:37
  31.5 39.2 %collective-permute-start.4 = (bf16[3,4,128,256]{2,3,1,0:T(8,128)(2,1)S(1)}, bf16[3,4,128,256]{2,3,1,0:T(8,128)(2,1)}, u32[]{:S(2)}, u32[]{:S(2)}) collective-permute-start(bf16[3,4,128,256]{2,3,1,0:T(8,128)(2,1)S(1)} %get-tuple-element.11), channel_id=1, source_target_pairs={{0,64},{8,72},{16,80},{24,88},{32,96},{40,104},{48,112},{56,120},{... | collective-permute-start | bytes 2359304 | tf_op jit(solution)/shard_map/ppermute | solution.py:37
  32.1 40.0 %collective-permute-start.5 = (bf16[3,4,128,256]{2,3,1,0:T(8,128)(2,1)S(1)}, bf16[3,4,128,256]{2,3,1,0:T(8,128)(2,1)}, u32[]{:S(2)}, u32[]{:S(2)}) collective-permute-start(bf16[3,4,128,256]{2,3,1,0:T(8,128)(2,1)S(1)} %get-tuple-element.11), channel_id=1, source_target_pairs={{0,32},{8,40},{16,48},{24,56},{32,64},{40,72},{48,80},{56,88},{64,... | collective-permute-start | bytes 2359304 | tf_op jit(solution)/shard_map/ppermute | solution.py:37
  48.2 3.4 %copy-start = (bf16[1024,2048]{1,0:T(8,128)(2,1)S(1)}, bf16[1024,2048]{1,0:T(8,128)(2,1)}, u32[]{:S(2)}) copy-start(bf16[1024,2048]{1,0:T(8,128)(2,1)} %all-gather.4.cloned.1.call-done) | copy-start | bytes 12582916
  127.0 21.9 %copy-start.3 = (bf16[1024,256]{1,0:T(8,128)(2,1)S(1)}, bf16[1024,256]{1,0:T(8,128)(2,1)}, u32[]{:S(2)}) copy-start(bf16[1024,256]{1,0:T(8,128)(2,1)} %shard_map.130) | copy-start | bytes 1572868
  152.3 0.7 copy-start.6
  152.3 137.7 %reduce-scatter.2.cloned.1.call-start = ((), (), s32[]{:S(2)}) async-start(), calls=%async_computation.3 | async-start | bytes 4718592 | tf_op jit(solution)/shard_map/reduce_scatter | solution.py:232
  224.6 5.6 %copy-start.2 = (bf16[2048,1024]{1,0:T(8,128)(2,1)S(1)}, bf16[2048,1024]{1,0:T(8,128)(2,1)}, u32[]{:S(2)}) copy-start(bf16[2048,1024]{1,0:T(8,128)(2,1)} %reshape_reshape.6) | copy-start | bytes 12582916
  230.2 6.4 %copy-start.1 = (bf16[1024,2048]{1,0:T(8,128)(2,1)}, bf16[1024,2048]{1,0:T(8,128)(2,1)S(1)}, u32[]{:S(2)}) copy-start(bf16[1024,2048]{1,0:T(8,128)(2,1)S(1)} %get-tuple-element.4) | copy-start | bytes 12582916
Sparse Core Ops, SparseCore 0:
  9.7 38.4 all-gather.3
  50.4 96.6 all-gather.5
  152.4 72.1 all-reduce.1
  252.1 37.8 reduce-scatter.1

commit v2 on v1

--- a/solution.py
+++ b/solution.py
@@ -68,11 +68,11 @@
         l_sc[...] = jnp.zeros(l_sc.shape, jnp.float32)
         acc_sc[...] = jnp.zeros(acc_sc.shape, jnp.float32)
 
-    def update(k_ref, v_ref, mask):
+    def update(keys_of, values_of, mask):
         for head in range(pair):
             lanes = pl.ds(head * HD, HD)
             q = q_ref[:, lanes] * scale
-            s = lax.dot_general(q, k_ref[:, lanes], (((1,), (1,)), ((), ())), preferred_element_type=jnp.float32)
+            s = lax.dot_general(q, keys_of(lanes), (((1,), (1,)), ((), ())), preferred_element_type=jnp.float32)
             if mask is not None:
                 s = jnp.where(mask, s, NEG_FILL)
             m_prev = m_sc[head]
@@ -83,26 +83,26 @@
                 p = jnp.where(mask, p, 0.0)
             l_sc[head] = alpha * l_sc[head] + jnp.sum(p, axis=1, keepdims=True)
             acc_sc[head] = alpha * acc_sc[head] + jnp.dot(
-                p.astype(jnp.bfloat16), v_ref[:, lanes], preferred_element_type=jnp.float32
+                p.astype(jnp.bfloat16), values_of(lanes), preferred_element_type=jnp.float32
             )
             m_sc[head] = m_new
 
     begin = j * tk
-
-    @pl.when((j < n_cache) & (begin + tk <= length))
+    in_cache = j < n_cache
+
+    @pl.when(jnp.logical_not(in_cache) | (begin < length))
     def _():
-        update(kc_ref, vc_ref, None)
-
-    @pl.when((j < n_cache) & (begin < length) & (begin + tk > length))
-    def _():
-        col = begin + lax.broadcasted_iota(jnp.int32, (tq, tk), 1)
-        update(kc_ref, vc_ref, col < length)
+        row = lax.broadcasted_iota(jnp.int32, (tq, tk), 0)
+        col = lax.broadcasted_iota(jnp.int32, (tq, tk), 1)
+        mask = col < jnp.where(in_cache, length - begin, row + 1)
+        update(
+            lambda lanes: jnp.where(in_cache, kc_ref[:, lanes], kn_ref[:, lanes]),
+            lambda lanes: jnp.where(in_cache, vc_ref[:, lanes], vn_ref[:, lanes]),
+            mask,
+        )
 
     @pl.when(j == n_cache)
     def _():
-        row = lax.broadcasted_iota(jnp.int32, (tq, tq), 0)
-        col = lax.broadcasted_iota(jnp.int32, (tq, tq), 1)
-        update(kn_ref, vn_ref, row >= col)
         for head in range(pair):
             o_ref[:, pl.ds(head * HD, HD)] = (acc_sc[head] / l_sc[head]).astype(o_ref.dtype)
 

time: 300 us -> 300 us (level)
  waiting for transfers between devices: 127 us -> 121 us
  Pallas kernels: 41.9 us -> 47.3 us
    pallas_call x1, Pallas kernels: 41.9 us -> 47.3 us  [flash_attention(): pl.pallas_call(body, grid_spec=grid_spec, out_shape=jax.ShapeDtypeStruct(...]
    all_gather x1, waiting for transfers between devices: 20.1 us -> 14.7 us  [gather_packed(): gathered = lax.all_gather(joined, axis_name, axis=0, tiled=False)]
  transfers between devices with their start and end apart: 10 -> 10, of which waited for: 8 -> 8; matrix products, arithmetic and copies ran while one was open for 23% -> 23% of each run, Pallas kernels for 14% -> 16%
where the time goes in v2:
time: 300 us; the launch traced here: 299 us
  waiting for transfers between devices  121 us (40%)
  local copies, waits for them, and re-layouts  48.9 us (16%)
  Pallas kernels  47.3 us (16%)
  matrix products  31.6 us (11%)
  other arithmetic  24.8 us (8%)
  between operations  14.6 us (5%)
  starting transfers between devices  10.3 us (3%)
    pallas_call x1, Pallas kernels, flash_attention(): pl.pallas_call(body, grid_spec=grid_spec, out_shape=jax.ShapeDtypeStruct(...  47.3 us
    psum x1, waiting for transfers between devices, on_device(): lax.psum(partial_value.astype(jnp.bfloat16), 'mp').astype(jnp.float32)  41.3 us
    reduce_scatter x1, waiting for transfers between devices, on_device(): lax.psum_scatter(terms.astype(jnp.bfloat16), 'mp', scatter_dimension=1, t...  38 us
    dot_general x1, matrix products, on_device(): terms = jnp.dot(units, w_down_full, preferred_element_type=jnp.float32)  15.4 us
    all_gather x1, waiting for transfers between devices, on_device(): full_rows = lax.all_gather(hidden_in, 'mp', axis=1, tiled=True)  15.1 us
    another operation x2, local copies, waits for them, and re-layouts, gather_packed(): outs.append(piece.reshape(shape))  14.7 us
    all_gather x1, waiting for transfers between devices, gather_packed(): gathered = lax.all_gather(joined, axis_name, axis=0, tiled=False)  14.7 us
    ppermute x3, waiting for transfers between devices, gather_req_shifted(): lax.ppermute(block, axis_name, inner(k))  9.82 us
  transfers between devices with their start and end apart: 10, of which 8 were waited for; matrix products, arithmetic and copies ran while one was open for 23% of the time, Pallas kernels for 16%

profile of v2, /device:TPU:0, one launch (start us, length us, event | category | flops | bytes accessed | tf_op | source)
XLA Modules:
  0.0 298.7 jit_solution(14015124434889921045)
XLA Ops:
  7.2 0.0 copy-start.4
  7.2 0.0 copy-start.5
  7.2 0.0 all-gather.4.cloned.1.call-start
  7.2 0.7 all-gather.4.cloned.1.call-update
  7.9 0.0 all-gather.6.cloned.1.call-start
  8.0 1.1 reshape.94
  9.0 1.1 reshape.95
  10.1 2.0 pad_maximum_fusion
  12.1 0.0 all-gather.6.cloned.1.call-update
  12.1 0.0 all-reduce.2.cloned.1.call-start
  12.1 0.0 copy-done.4
  12.1 0.2 copy.33
  12.3 4.2 %collective-permute-start = (bf16[3,128,256]{1,2,0:T(8,128)(2,1)S(1)}, bf16[3,128,256]{1,2,0:T(8,128)(2,1)S(1)}, u32[]{:S(2)}, u32[]{:S(2)}) collective-permute-start(bf16[3,128,256]{1,2,0:T(8,128)(2,1)S(1)} %copy.33), channel_id=1, source_target_pairs={{0,24},{8,0},{16,8},{24,16},{32,56},{40,32},{48,40},{56,48},{64,88... | collective-permute-start | bytes 589832 | tf_op jit(solution)/shard_map/ppermute | solution.py:35
  16.5 0.0 collective-permute-start.1
  16.5 1.3 collective-permute-start.2
  17.8 0.0 copy-done.5
  18.5 6.4 %collective-permute-done = bf16[3,128,256]{1,2,0:T(8,128)(2,1)S(1)} collective-permute-done((bf16[3,128,256]{1,2,0:T(8,128)(2,1)S(1)}, bf16[3,128,256]{1,2,0:T(8,128)(2,1)S(1)}, u32[]{:S(2)}, u32[]{:S(2)}) %collective-permute-start) | collective-permute-done | bytes 196640 | tf_op jit(solution)/shard_map/ppermute | solution.py:35
  24.9 1.0 collective-permute-done.1
  25.8 2.5 collective-permute-done.2
  28.3 0.1 fusion.53
  28.4 3.1 %collective-permute-start.3 = (bf16[3,4,128,256]{2,3,1,0:T(8,128)(2,1)S(1)}, bf16[3,4,128,256]{2,3,1,0:T(8,128)(2,1)S(1)}, u32[]{:S(2)}, u32[]{:S(2)}) collective-permute-start(bf16[3,4,128,256]{2,3,1,0:T(8,128)(2,1)S(1)} %get-tuple-element.11), channel_id=1, source_target_pairs={{0,96},{8,104},{16,112},{24,120},{32,0},{40,8},{48,16},{56,24},{64... | collective-permute-start | bytes 2359304 | tf_op jit(solution)/shard_map/ppermute | solution.py:37
  31.5 0.6 collective-permute-start.4
  32.1 1.0 collective-permute-start.5
  33.1 15.1 %all-gather.4.cloned.1.call-done = bf16[1024,2048]{1,0:T(8,128)(2,1)} async-done(((bf16[1024,256]{1,0:T(8,128)(2,1)}), bf16[1024,2048]{1,0:T(8,128)(2,1)}) %all-gather.4.cloned.1.call-update) | async-done | bytes 4194320 | tf_op jit(solution)/shard_map/all_gather | solution.py:171
  48.2 0.0 copy-start
  48.2 3.2 %fusion.3 = f32[1024]{0:T(1024)S(1)} fusion(bf16[1024,2048]{1,0:T(8,128)(2,1)} %all-gather.4.cloned.1.call-done), kind=kLoop, calls=%fused_computation.8 | loop fusion | flops 6290432 | bytes 4198400 | tf_op jit(solution)/shard_map/reduce_sum | solution.py:19
  51.5 0.2 copy-done
  51.7 3.0 %fusion.5 = bf16[1024,2048]{1,0:T(8,128)(2,1)} fusion(bf16[1024,2048]{1,0:T(8,128)(2,1)S(1)} %copy-done, f32[2048]{0:T(1024)S(1)} %convert_element_type.68, f32[1024]{0:T(1024)S(1)} %add_rsqrt_fusion.1), kind=kLoop, calls=%fused_computation.10 | loop fusion | flops 8388608 | bytes 8400896 | tf_op jit(solution)/shard_map/convert_element_type | solution.py:20
  54.7 6.4 %copy.37 = bf16[1024,2048]{0,1:T(8,128)(2,1)} copy(bf16[1024,2048]{1,0:T(8,128)(2,1)} %fusion.5) | data formatting | bytes 8388608 | tf_op jit(solution)/shard_map/convert_element_type | solution.py:20
  61.1 6.4 %copy.38 = bf16[1024,4,4,128]{3,0,2,1:T(8,128)(2,1)} copy(bf16[1024,4,4,128]{0,3,2,1:T(8,128)(2,1)} %bitcast.59) | data formatting | bytes 8388608 | tf_op jit(solution)/shard_map/reshape | solution.py:173
  67.5 3.1 %fusion.11 = bf16[1024,4,4,128]{3,0,2,1:T(8,128)(2,1)S(1)} fusion(s32[]{:T(128)S(6)} %select_n.82, bf16[1024,4,4,128]{3,0,2,1:T(8,128)(2,1)} %copy.38), kind=kLoop, calls=%fused_computation.19 | loop fusion | flops 2097152 | bytes 8388612 | tf_op jit(solution)/shard_map/jit(_roll_dynamic)/concatenate | solution.py:174
  70.6 0.0 collective-permute-done.3
  70.6 0.0 collective-permute-done.4
  70.7 1.4 collective-permute-done.5
  72.1 5.4 %fusion.19 = f32[3,1024,256]{2,1,0:T(8,128)S(1)} fusion(s32[]{:T(128)S(6)} %select_n.85, bf16[1024,4,4,128]{3,0,2,1:T(8,128)(2,1)S(1)} %fusion.11, bf16[3,1,4,128,256]{3,4,2,0,1:T(8,128)(2,1)} %bitcast.7, bf16[3,1,4,128,256]{3,4,2,0,1:T(8,128)(2,1)} %bitcast.6, bf16[3,1,4,128,256]{3,4,2,0,1:T(8,128)(2,1)S(1)} %bitcast.70, ...), kind=kOutput, calls=%fused_computation.31 | convolution fusion | flops 3228041216 | bytes 10485764 | tf_op jit(solution)/shard_map/nd,kdw->knw/dot_general | solution.py:175
  77.5 0.8 fusion.38.vn_ref
  78.4 1.2 fusion.40
  79.5 5.6 %fusion.34 = (bf16[1024,256]{1,0:T(8,128)(2,1)}, bf16[1024,256]{1,0:T(8,128)(2,1)}) fusion(f32[2,1024,256]{2,1,0:T(8,128)S(1)} %fusion.40, f32[3,1024,256]{2,1,0:T(8,128)S(1)} %fusion.19, f32[256]{0:T(256)S(1)} %get-tuple-element.12, f32[256]{0:T(256)S(1)} %get-tuple-element.13, f32[1024]{0:T(1024)S(1)} %add_convert_fusion.1), kind=kLoop, calls=%fused_computation.40 | loop fusion | flops 2621440 | bytes 5249024 | tf_op jit(solution)/shard_map/convert_element_type | solution.py:199
  85.1 47.3 %shard_map.130 = bf16[1024,256]{1,0:T(8,128)(2,1)} custom-call(s32[1]{0:T(128)} %copy.47.len_ref, bf16[1024,256]{1,0:T(8,128)(2,1)} %get-tuple-element.9.q_ref, bf16[4096,256]{1,0:T(8,128)(2,1)} %bitcast.68, bf16[4096,256]{1,0:T(8,128)(2,1)} %bitcast.69, bf16[1024,256]{1,0:T(8,128)(2,1)} %get-tuple-element.8.kn_ref, bf16[1024,256]{1,0:T(8,128)(2,1)} %fusion.38.vn_ref), custom_call_target="tpu_custom_call" | custom-call | flops 5368709120 | bytes 6291456 | tf_op jit(solution)/shard_map/pallas_call | solution.py:147
  132.4 0.0 copy-start.3
  132.4 14.7 %all-gather.6.cloned.1.call-done = bf16[53248,128]{1,0:T(8,128)(2,1)} async-done(((bf16[3328,128]{1,0:T(8,128)(2,1)}), bf16[53248,128]{1,0:T(8,128)(2,1)}) %all-gather.6.cloned.1.call-update) | async-done | bytes 13631504 | tf_op jit(solution)/shard_map/all_gather | solution.py:45
  147.1 1.3 slice_bitcast_fusion.1
  148.4 0.5 copy.41
  149.0 0.0 copy-done.3
  149.0 3.3 %convolution_convert_fusion = bf16[1024,2048]{1,0:T(8,128)(2,1)} fusion(bf16[1024,256]{1,0:T(8,128)(2,1)S(1)} %copy-done.3, bf16[256,2048]{0,1:T(8,128)(2,1)S(1)} %bitcast.62), kind=kOutput, calls=%fused_computation.22 | convolution fusion | flops 1075838976 | bytes 5767168 | tf_op jit(solution)/shard_map/dot_general | solution.py:211
  152.3 0.0 copy-start.6
  152.3 0.0 all-reduce.2.cloned.1.call-update
  152.3 0.0 reduce-scatter.2.cloned.1.call-start
  152.3 0.6 copy-done.6
  153.0 9.1 %fusion.55 = (bf16[16,1024,128]{2,1,0:T(8,128)(2,1)}, bf16[1024,16,128]{2,0,1:T(8,128)(2,1)}, bf16[16,1024,128]{2,1,0:T(8,128)(2,1)}) fusion(bf16[16,3328,128]{2,1,0:T(8,128)(2,1)} %bitcast.61), kind=kLoop, calls=%fused_computation.80 | loop fusion | bytes 25165824 | tf_op jit(solution)/shard_map/slice | solution.py:50
  162.1 7.4 %reshape_reshape.6 = bf16[2048,1024]{1,0:T(8,128)(2,1)} reshape(bf16[16,1024,128]{2,1,0:T(8,128)(2,1)} %get-tuple-element.7) | data formatting | bytes 8388608 | tf_op jit(solution)/shard_map/reshape;reshape | solution.py:54
  169.5 6.4 %copy.42 = bf16[1024,16,128]{0,2,1:T(8,128)(2,1)} copy(bf16[1024,16,128]{2,0,1:T(8,128)(2,1)} %get-tuple-element.6) | data formatting | bytes 8388608 | tf_op jit(solution)/shard_map/transpose | solution.py:51
  175.9 7.4 %reshape_reshape.7 = bf16[2048,1024]{1,0:T(8,128)(2,1)} reshape(bf16[16,1024,128]{2,1,0:T(8,128)(2,1)} %get-tuple-element.5) | data formatting | bytes 8388608 | tf_op jit(solution)/shard_map/reshape;reshape | solution.py:54
  183.3 41.3 %all-reduce.2.cloned.1.call-done = bf16[1024,2048]{1,0:T(8,128)(2,1)} async-done(((bf16[1024,2048]{1,0:T(8,128)(2,1)}), bf16[1024,2048]{1,0:T(8,128)(2,1)}) %all-reduce.2.cloned.1.call-update) | async-done | bytes 4194320 | tf_op jit(solution)/shard_map/psum | solution.py:214
  224.6 0.0 copy-start.2
  224.6 5.6 %fusion = (f32[1024]{0:T(1024)S(1)}, bf16[1024,2048]{1,0:T(8,128)(2,1)S(1)}) fusion(bf16[1024,2048]{1,0:T(8,128)(2,1)} %all-reduce.2.cloned.1.call-done, bf16[1024,2048]{1,0:T(8,128)(2,1)} %all-gather.4.cloned.1.call-done), kind=kLoop, calls=%fused_computation.5 | loop fusion | flops 14679040 | bytes 12587008 | tf_op jit(solution)/shard_map/reduce_sum | solution.py:19
  230.2 0.0 copy-start.1
  230.2 0.0 copy-done.2
  230.3 6.3 %fusion.27 = f32[1024,1024]{1,0:T(8,128)} fusion(bf16[2048,1024]{1,0:T(8,128)(2,1)S(1)} %copy-done.2, bf16[1024,2048]{1,0:T(8,128)(2,1)S(1)} %get-tuple-element.4, f32[2048]{0:T(1024)S(1)} %convert_element_type.80, f32[1024]{0:T(1024)S(1)} %add_rsqrt_fusion), kind=kOutput, calls=%fused_computation.36 | convolution fusion | flops 4303355904 | bytes 12595200 | tf_op jit(solution)/shard_map/dot_general | solution.py:220
  236.6 0.0 copy-done.1
  236.6 15.4 %convolution_convert_fusion.1 = bf16[1024,2048]{1,0:T(8,128)(2,1)} fusion(bf16[1024,2048]{0,1:T(8,128)(2,1)} %bitcast.63, f32[1024,1024]{1,0:T(8,128)} %fusion.27, bf16[2048,1024]{1,0:T(8,128)(2,1)} %reshape_reshape.7, bf16[1024,2048]{1,0:T(8,128)(2,1)} %copy-done.1, f32[2048]{0:T(1024)S(1)} %convert_element_type.80, f32[1024]{0:T(1024)S(1)} %add_rsqrt_fusion), kind=kOutput, calls=%fused_computation.23 | convolution fusion | flops 8606711808 | bytes 20983808 | tf_op jit(solution)/shard_map/dot_general | solution.py:229
  252.0 0.0 reduce-scatter.2.cloned.1.call-update
  252.0 38.0 %reduce-scatter.2.cloned.1.call-done = bf16[1024,256]{1,0:T(8,128)(2,1)} async-done(((bf16[1024,2048]{1,0:T(8,128)(2,1)}), bf16[1024,256]{1,0:T(8,128)(2,1)}) %reduce-scatter.2.cloned.1.call-update) | async-done | bytes 524304 | tf_op jit(solution)/shard_map/reduce_scatter | solution.py:232
  290.0 2.1 add_convert_fusion
  (7 shorter events, 0.0 us)
Async XLA Ops:
  7.2 5.0 %copy-start.4 = (bf16[3,128,256]{2,1,0:T(8,128)(2,1)S(1)}, bf16[3,128,256]{2,1,0:T(8,128)(2,1)}, u32[]{:S(2)}) copy-start(bf16[3,128,256]{2,1,0:T(8,128)(2,1)} %param.12) | copy-start | bytes 589828
  7.2 10.6 %copy-start.5 = (bf16[2048]{0:T(1024)(128)(2,1)S(1)}, bf16[2048]{0:T(1024)(128)(2,1)}, u32[]{:S(2)}) copy-start(bf16[2048]{0:T(1024)(128)(2,1)} %param.14) | copy-start | bytes 12292
  7.2 41.0 %all-gather.4.cloned.1.call-start = ((), (), s32[]{:S(2)}) async-start(), calls=%async_computation.1 | async-start | bytes 4718592 | tf_op jit(solution)/shard_map/all_gather | solution.py:171
  7.9 139.2 %all-gather.6.cloned.1.call-start = ((), (), s32[]{:S(2)}) async-start(), calls=%async_computation.4 | async-start | bytes 14483456 | tf_op jit(solution)/shard_map/all_gather | solution.py:45
  12.1 212.5 %all-reduce.2.cloned.1.call-start = ((), (), s32[]{:S(2)}) async-start(), calls=%async_computation.2 | async-start | bytes 8388608 | tf_op jit(solution)/shard_map/psum | solution.py:214
  12.3 12.6 %collective-permute-start = (bf16[3,128,256]{1,2,0:T(8,128)(2,1)S(1)}, bf16[3,128,256]{1,2,0:T(8,128)(2,1)S(1)}, u32[]{:S(2)}, u32[]{:S(2)}) collective-permute-start(bf16[3,128,256]{1,2,0:T(8,128)(2,1)S(1)} %copy.33), channel_id=1, source_target_pairs={{0,24},{8,0},{16,8},{24,16},{32,56},{40,32},{48,40},{56,48},{64,88... | collective-permute-start | bytes 589832 | tf_op jit(solution)/shard_map/ppermute | solution.py:35
  16.5 9.3 %collective-permute-start.1 = (bf16[3,128,256]{1,2,0:T(8,128)(2,1)S(1)}, bf16[3,128,256]{1,2,0:T(8,128)(2,1)S(1)}, u32[]{:S(2)}, u32[]{:S(2)}) collective-permute-start(bf16[3,128,256]{1,2,0:T(8,128)(2,1)S(1)} %copy.33), channel_id=1, source_target_pairs={{0,16},{8,24},{16,0},{24,8},{32,48},{40,56},{48,32},{56,40},{64,80... | collective-permute-start | bytes 589832 | tf_op jit(solution)/shard_map/ppermute | solution.py:35
  16.5 11.8 %collective-permute-start.2 = (bf16[3,128,256]{1,2,0:T(8,128)(2,1)S(1)}, bf16[3,128,256]{1,2,0:T(8,128)(2,1)S(1)}, u32[]{:S(2)}, u32[]{:S(2)}) collective-permute-start(bf16[3,128,256]{1,2,0:T(8,128)(2,1)S(1)} %copy.33), channel_id=1, source_target_pairs={{0,8},{8,16},{16,24},{24,0},{32,40},{40,48},{48,56},{56,32},{64,72... | collective-permute-start | bytes 589832 | tf_op jit(solution)/shard_map/ppermute | solution.py:35
  28.4 42.2 %collective-permute-start.3 = (bf16[3,4,128,256]{2,3,1,0:T(8,128)(2,1)S(1)}, bf16[3,4,128,256]{2,3,1,0:T(8,128)(2,1)S(1)}, u32[]{:S(2)}, u32[]{:S(2)}) collective-permute-start(bf16[3,4,128,256]{2,3,1,0:T(8,128)(2,1)S(1)} %get-tuple-element.11), channel_id=1, source_target_pairs={{0,96},{8,104},{16,112},{24,120},{32,0},{40,8},{48,16},{56,24},{64... | collective-permute-start | bytes 2359304 | tf_op jit(solution)/shard_map/ppermute | solution.py:37
  31.5 39.2 %collective-permute-start.4 = (bf16[3,4,128,256]{2,3,1,0:T(8,128)(2,1)S(1)}, bf16[3,4,128,256]{2,3,1,0:T(8,128)(2,1)}, u32[]{:S(2)}, u32[]{:S(2)}) collective-permute-start(bf16[3,4,128,256]{2,3,1,0:T(8,128)(2,1)S(1)} %get-tuple-element.11), channel_id=1, source_target_pairs={{0,64},{8,72},{16,80},{24,88},{32,96},{40,104},{48,112},{56,120},{... | collective-permute-start | bytes 2359304 | tf_op jit(solution)/shard_map/ppermute | solution.py:37
  32.1 40.0 %collective-permute-start.5 = (bf16[3,4,128,256]{2,3,1,0:T(8,128)(2,1)S(1)}, bf16[3,4,128,256]{2,3,1,0:T(8,128)(2,1)}, u32[]{:S(2)}, u32[]{:S(2)}) collective-permute-start(bf16[3,4,128,256]{2,3,1,0:T(8,128)(2,1)S(1)} %get-tuple-element.11), channel_id=1, source_target_pairs={{0,32},{8,40},{16,48},{24,56},{32,64},{40,72},{48,80},{56,88},{64,... | collective-permute-start | bytes 2359304 | tf_op jit(solution)/shard_map/ppermute | solution.py:37
  48.2 3.4 %copy-start = (bf16[1024,2048]{1,0:T(8,128)(2,1)S(1)}, bf16[1024,2048]{1,0:T(8,128)(2,1)}, u32[]{:S(2)}) copy-start(bf16[1024,2048]{1,0:T(8,128)(2,1)} %all-gather.4.cloned.1.call-done) | copy-start | bytes 12582916
  132.4 16.6 %copy-start.3 = (bf16[1024,256]{1,0:T(8,128)(2,1)S(1)}, bf16[1024,256]{1,0:T(8,128)(2,1)}, u32[]{:S(2)}) copy-start(bf16[1024,256]{1,0:T(8,128)(2,1)} %shard_map.130) | copy-start | bytes 1572868
  152.3 0.7 copy-start.6
  152.3 137.7 %reduce-scatter.2.cloned.1.call-start = ((), (), s32[]{:S(2)}) async-start(), calls=%async_computation.3 | async-start | bytes 4718592 | tf_op jit(solution)/shard_map/reduce_scatter | solution.py:232
  224.6 5.6 %copy-start.2 = (bf16[2048,1024]{1,0:T(8,128)(2,1)S(1)}, bf16[2048,1024]{1,0:T(8,128)(2,1)}, u32[]{:S(2)}) copy-start(bf16[2048,1024]{1,0:T(8,128)(2,1)} %reshape_reshape.6) | copy-start | bytes 12582916
  230.2 6.4 %copy-start.1 = (bf16[1024,2048]{1,0:T(8,128)(2,1)}, bf16[1024,2048]{1,0:T(8,128)(2,1)S(1)}, u32[]{:S(2)}) copy-start(bf16[1024,2048]{1,0:T(8,128)(2,1)S(1)} %get-tuple-element.4) | copy-start | bytes 12582916
Sparse Core Ops, SparseCore 0:
  9.7 38.4 all-gather.3
  50.4 96.6 all-gather.5
  152.4 72.1 all-reduce.1
  252.1 37.8 reduce-scatter.1

commit v3 on v2

--- a/solution.py
+++ b/solution.py
@@ -168,10 +168,35 @@
     width = w_qkv.shape[2]
     heads_local = width // HD
     slots = k_cache.shape[1]
-    full_rows = lax.all_gather(hidden_in, "mp", axis=1, tiled=True)
-    normed = rms_scale(full_rows, attn_gain)
-    blocks = normed.reshape(new_count, side, side, -1)
-    columns = jnp.roll(blocks, (-row, -col), axis=(1, 2)).reshape(new_count, -1)
+    n_mp = lax.axis_size("mp")
+    chips = n_mp // 2
+    mine = lax.axis_index("mp")
+    chip, core = mine // 2, mine % 2
+    pair_perm = [(s, s ^ 1) for s in range(n_mp)]
+    remote = [
+        lax.ppermute(hidden_in, "mp", [(s, (s - 2 * dx) % n_mp) for s in range(n_mp)])
+        for dx in range(1, chips)
+    ]
+    sibling = lax.ppermute(hidden_in, "mp", pair_perm)
+    sibling_remote = lax.ppermute(jnp.stack(remote), "mp", pair_perm)
+    pieces = [hidden_in, sibling]
+    for dx in range(chips - 1):
+        pieces += [remote[dx], sibling_remote[dx]]
+    lane = 128
+    per_piece = hidden_in.shape[1] // lane
+    held = jnp.concatenate([piece.reshape(new_count, per_piece, lane) for piece in pieces], axis=1)
+
+    def held_index(block):
+        owner = block // per_piece
+        return (((owner // 2 - chip) % chips) * 2 + (owner % 2 ^ core)) * per_piece + block % per_piece
+
+    n_blocks = side * side
+    order = jnp.arange(n_blocks, dtype=jnp.int32)
+    wanted = ((row + order // side) % side) * side + (col + order % side) % side
+    hidden_cols = jnp.take(held, held_index(wanted), axis=1).reshape(new_count, -1)
+    gain_cols = jnp.take(attn_gain.reshape(n_blocks, lane), wanted, axis=0).reshape(-1)
+    columns = rms_scale(hidden_cols, gain_cols)
+    full_rows = jnp.take(held, held_index(order), axis=1).reshape(new_count, -1)
     projected = jnp.einsum(
         "nd,kdw->knw",
         columns,

time: 300 us -> 393 us (1.31)
  waiting for transfers between devices: 121 us -> 166 us
  local copies, waits for them, and re-layouts: 48.9 us -> 87.1 us
  starting transfers between devices: 10.3 us -> 18.1 us
    ppermute x3, waiting for transfers between devices: 1.45 us -> 53 us  [gather_req_shifted(): lax.ppermute(stage, axis_name, outer(k))]
    all_gather x1 -> x0, waiting for transfers between devices: 15.1 us -> none  [on_device(): full_rows = lax.all_gather(hidden_in, 'mp', axis=1, tiled=True)]
    ppermute x0 -> x5, waiting for transfers between devices: none -> 15.1 us  [the longest x3 15.1 us: on_device(): lax.ppermute(hidden_in, 'mp', [(s, (s - 2 * dx) % n_mp) for s in range(n_...]
    all_gather x1, waiting for transfers between devices: 14.7 us -> 0.01 us  [gather_packed(): gathered = lax.all_gather(joined, axis_name, axis=0, tiled=False)]
    psum x1, waiting for transfers between devices: 41.3 us -> 53.2 us  [on_device(): lax.psum(partial_value.astype(jnp.bfloat16), 'mp').astype(jnp.float32)]
    gather x0 -> x3, local copies, waits for them, and re-layouts: none -> 11.1 us  [the longest x1 5.31 us: on_device(): full_rows = jnp.take(held, held_index(order), axis=1).reshape(new_count, -1)]
    unnamed x15 -> x28, local copies, waits for them, and re-layouts: 1.01 us -> 12.1 us
    another operation x0 -> x4, local copies, waits for them, and re-layouts: none -> 10.5 us  [the longest x3 6.13 us: on_device(): piece.reshape(new_count, per_piece, lane)]
  transfers between devices with their start and end apart: 10 -> 14, of which waited for: 8 -> 8; matrix products, arithmetic and copies ran while one was open for 23% -> 27% of each run, Pallas kernels for 16% -> 12%
where the time goes in v3:
time: 393 us; the launch traced here: 391 us
  waiting for transfers between devices  166 us (42%)
  local copies, waits for them, and re-layouts  87.1 us (22%)
  Pallas kernels  47.3 us (12%)
  matrix products  31.7 us (8%)
  other arithmetic  26.6 us (7%)
  starting transfers between devices  18.1 us (5%)
  between operations  14.6 us (4%)
    psum x1, waiting for transfers between devices, on_device(): lax.psum(partial_value.astype(jnp.bfloat16), 'mp').astype(jnp.float32)  53.2 us
    ppermute x3, waiting for transfers between devices, gather_req_shifted(): lax.ppermute(stage, axis_name, outer(k))  53 us
    pallas_call x1, Pallas kernels, flash_attention(): pl.pallas_call(body, grid_spec=grid_spec, out_shape=jax.ShapeDtypeStruct(...  47.3 us
    reduce_scatter x1, waiting for transfers between devices, on_device(): lax.psum_scatter(terms.astype(jnp.bfloat16), 'mp', scatter_dimension=1, t...  38.1 us
    dot_general x1, matrix products, on_device(): terms = jnp.dot(units, w_down_full, preferred_element_type=jnp.float32)  15.4 us
    ppermute x3, waiting for transfers between devices, on_device(): lax.ppermute(hidden_in, 'mp', [(s, (s - 2 * dx) % n_mp) for s in range(n_...  15.1 us
    another operation x2, local copies, waits for them, and re-layouts, gather_packed(): outs.append(piece.reshape(shape))  14.7 us
    unnamed x28, local copies, waits for them, and re-layouts  12.1 us
  transfers between devices with their start and end apart: 14, of which 8 were waited for; matrix products, arithmetic and copies ran while one was open for 27% of the time, Pallas kernels for 12%

profile of v3, /device:TPU:0, one launch (start us, length us, event | category | flops | bytes accessed | tf_op | source)
XLA Modules:
  0.0 391.5 jit_solution(529343106307271016)
XLA Ops:
  7.2 1.1 reshape.287
  8.3 1.1 reshape.288
  9.4 2.0 pad_maximum_fusion.2
  11.4 1.2 copy.19
  12.7 2.9 collective-permute-start.1
  15.6 0.8 collective-permute-start.2
  16.4 0.9 collective-permute-start.3
  17.3 4.0 %collective-permute-start.5 = (bf16[3,128,256]{2,1,0:T(8,128)(2,1)S(1)}, bf16[3,128,256]{2,1,0:T(8,128)(2,1)S(1)}, u32[]{:S(2)}, u32[]{:S(2)}) collective-permute-start(bf16[3,128,256]{2,1,0:T(8,128)(2,1)S(1)} %copy-done.8), channel_id=1, source_target_pairs={{0,24},{8,0},{16,8},{24,16},{32,56},{40,32},{48,40},{56,48},{64,88... | collective-permute-start | bytes 589832 | tf_op jit(solution)/shard_map/ppermute | solution.py:35
  22.4 0.6 gather_fusion
  22.9 15.1 %collective-permute-done.1 = bf16[1024,256]{0,1:T(8,128)(2,1)S(1)} collective-permute-done((bf16[1024,256]{0,1:T(8,128)(2,1)S(1)}, bf16[1024,256]{0,1:T(8,128)(2,1)S(1)}, u32[]{:S(2)}, u32[]{:S(2)}) %collective-permute-start.1) | collective-permute-done | bytes 524320 | tf_op jit(solution)/shard_map/ppermute | solution.py:177
  38.0 3.9 collective-permute-start.6
  41.9 1.0 collective-permute-start.7
  43.0 1.3 pad_maximum_fusion.1
  44.4 4.7 %collective-permute-done.6 = bf16[3,128,256]{2,1,0:T(8,128)(2,1)S(1)} collective-permute-done((bf16[3,128,256]{2,1,0:T(8,128)(2,1)S(1)}, bf16[3,128,256]{2,1,0:T(8,128)(2,1)S(1)}, u32[]{:S(2)}, u32[]{:S(2)}) %collective-permute-start.6) | collective-permute-done | bytes 196640 | tf_op jit(solution)/shard_map/ppermute | solution.py:35
  49.0 1.9 collective-permute-done.7
  50.9 1.3 fusion.57
  52.3 2.7 collective-permute-start.8
  55.0 0.8 collective-permute-start.9
  55.8 0.9 collective-permute-start.10
  56.7 0.8 constant_dynamic-update-slice_fusion.7
  57.6 1.3 copy.25
  59.2 1.0 copy.28
  60.3 1.0 copy.30
  61.3 0.9 constant_dynamic-update-slice_fusion.6
  62.1 0.8 constant_dynamic-update-slice_fusion.5
  63.0 28.5 %collective-permute-done.8 = bf16[3,4,128,256]{3,2,0,1:T(8,128)(2,1)S(1)} collective-permute-done((bf16[3,4,128,256]{3,2,0,1:T(8,128)(2,1)}, bf16[3,4,128,256]{3,2,0,1:T(8,128)(2,1)S(1)}, u32[]{:S(2)}, u32[]{:S(2)}) %collective-permute-start.8) | collective-permute-done | bytes 786464 | tf_op jit(solution)/shard_map/ppermute | solution.py:37
  91.4 0.7 collective-permute-done.9
  92.1 23.9 %collective-permute-done.10 = bf16[3,4,128,256]{3,2,0,1:T(8,128)(2,1)} collective-permute-done((bf16[3,4,128,256]{3,2,0,1:T(8,128)(2,1)}, bf16[3,4,128,256]{3,2,0,1:T(8,128)(2,1)}, u32[]{:S(2)}, u32[]{:S(2)}) %collective-permute-start.10) | collective-permute-done | bytes 786464 | tf_op jit(solution)/shard_map/ppermute | solution.py:37
  116.0 2.2 pad_maximum_fusion
  118.2 4.4 %copy.33 = bf16[3,4,4,128,256]{3,2,1,4,0:T(4,128)(2,1)} copy(bf16[3,4,4,128,256]{4,3,0,2,1:T(8,128)(2,1)S(1)} %pad_maximum_fusion) | data formatting | bytes 6291456 | tf_op jit(solution)/shard_map/stack | solution.py:38
  122.5 4.8 %reshape.285 = bf16[3,2048,256]{1,2,0:T(8,128)(2,1)S(1)} reshape(bf16[3,4,4,128,256]{3,2,1,4,0:T(4,128)(2,1)} %copy.33) | data formatting | bytes 6291456 | tf_op jit(solution)/shard_map/reshape | solution.py:164
  127.3 2.5 fusion.60
  129.9 2.0 copy.27
  131.9 2.0 copy.29
  133.9 2.0 copy.31
  136.0 1.9 constant_dynamic-update-slice_fusion.4
  137.9 1.9 constant_dynamic-update-slice_fusion.3
  139.8 1.9 constant_dynamic-update-slice_fusion.2
  141.7 1.9 constant_dynamic-update-slice_fusion.1
  143.6 0.8 constant_dynamic-update-slice_fusion
  144.4 5.2 %gather_fusion.2 = bf16[16,1024,128]{2,1,0:T(8,128)(2,1)} fusion(bf16[1024,16,128]{2,0,1:T(8,128)(2,1)} %constant_dynamic-update-slice_fusion, s32[1024]{0:T(1024)S(1)} %pad_clamp_fusion.1), kind=kCustom, calls=%fused_computation.1.clone | custom fusion | bytes 8388672 | tf_op jit(solution)/shard_map/jit(_take)/gather | solution.py:196
  149.7 3.6 fusion
  153.3 3.6 fusion.2
  156.9 6.4 %copy.34 = bf16[1024,16,128]{0,2,1:T(8,128)(2,1)} copy(bf16[1024,16,128]{2,0,1:T(8,128)(2,1)} %fusion.2) | data formatting | bytes 8388608 | tf_op jit(solution)/shard_map/convert_element_type | solution.py:20
  163.3 5.6 %convolution_bitcast_fusion = f32[3,1024,256]{2,1,0:T(8,128)S(1)} fusion(bf16[3,2048,256]{1,2,0:T(8,128)(2,1)S(1)} %reshape.285, bf16[1024,2048,1]{0,1,2:T(8,128)(2,1)} %bitcast.89), kind=kOutput, calls=%fused_computation.22 | convolution fusion | flops 3221225472 | bytes 10485760 | tf_op jit(solution)/shard_map/nd,kdw->knw/dot_general | solution.py:200
  168.9 0.8 fusion.21.vn_ref
  169.7 1.1 fusion.23
  170.8 5.6 %fusion.17 = (bf16[1024,256]{1,0:T(8,128)(2,1)}, bf16[1024,256]{1,0:T(8,128)(2,1)}) fusion(f32[2,1024,256]{2,1,0:T(8,128)S(1)} %fusion.23, f32[3,1024,256]{2,1,0:T(8,128)S(1)} %convolution_bitcast_fusion, f32[256]{0:T(256)S(1)} %get-tuple-element.23, f32[256]{0:T(256)S(1)} %get-tuple-element.24, f32[1024]{0:T(1024)S(1)} %add_convert_fusion.1), kind=kLoop, calls=%fused_computation.32 | loop fusion | flops 2621440 | bytes 5249024 | tf_op jit(solution)/shard_map/convert_element_type | solution.py:224
  176.4 47.3 %shard_map.130 = bf16[1024,256]{1,0:T(8,128)(2,1)} custom-call(s32[1]{0:T(128)} %copy.53.len_ref, bf16[1024,256]{1,0:T(8,128)(2,1)} %get-tuple-element.14.q_ref, bf16[4096,256]{1,0:T(8,128)(2,1)} %bitcast.105, bf16[4096,256]{1,0:T(8,128)(2,1)} %bitcast.106, bf16[1024,256]{1,0:T(8,128)(2,1)} %get-tuple-element.13.kn_ref, bf16[1024,256]{1,0:T(8,128)(2,1)} %fusion.21.vn_ref), custom_call_target="tpu_custom_call" | custom-call | flops 5368709120 | bytes 6291456 | tf_op jit(solution)/shard_map/pallas_call | solution.py:147
  223.7 1.4 slice_bitcast_fusion.1
  225.0 0.5 copy.37
  225.6 3.3 convolution_convert_fusion
  229.0 0.6 copy-done.9
  229.6 5.3 %gather_fusion.1 = bf16[16,1024,128]{2,1,0:T(8,128)(2,1)} fusion(bf16[1024,16,128]{2,0,1:T(8,128)(2,1)} %constant_dynamic-update-slice_fusion, s32[1024]{0:T(1024)S(1)} %get-tuple-element.22), kind=kCustom, calls=%fused_computation.clone | custom fusion | bytes 8388672 | tf_op jit(solution)/shard_map/jit(_take)/gather | solution.py:199
  234.9 9.0 %fusion.59 = (bf16[16,1024,128]{2,1,0:T(8,128)(2,1)}, bf16[1024,16,128]{2,0,1:T(8,128)(2,1)}, bf16[16,1024,128]{2,1,0:T(8,128)(2,1)}) fusion(bf16[16,3328,128]{2,1,0:T(8,128)(2,1)} %bitcast.86), kind=kLoop, calls=%fused_computation.159 | loop fusion | bytes 25165824 | tf_op jit(solution)/shard_map/slice | solution.py:50
  243.9 7.3 %reshape_reshape.6 = bf16[2048,1024]{1,0:T(8,128)(2,1)} reshape(bf16[16,1024,128]{2,1,0:T(8,128)(2,1)} %get-tuple-element.12) | data formatting | bytes 8388608 | tf_op jit(solution)/shard_map/reshape;reshape | solution.py:54
  251.3 6.4 %copy.38 = bf16[1024,16,128]{0,2,1:T(8,128)(2,1)} copy(bf16[1024,16,128]{2,0,1:T(8,128)(2,1)} %get-tuple-element.11) | data formatting | bytes 8388608 | tf_op jit(solution)/shard_map/transpose | solution.py:51
  257.7 7.4 %reshape_reshape.7 = bf16[2048,1024]{1,0:T(8,128)(2,1)} reshape(bf16[16,1024,128]{2,1,0:T(8,128)(2,1)} %get-tuple-element.10) | data formatting | bytes 8388608 | tf_op jit(solution)/shard_map/reshape;reshape | solution.py:54
  265.0 53.2 %all-reduce.2.cloned.1.call-done = bf16[1024,2048]{1,0:T(8,128)(2,1)} async-done(((bf16[1024,2048]{1,0:T(8,128)(2,1)}), bf16[1024,2048]{1,0:T(8,128)(2,1)}) %all-reduce.2.cloned.1.call-update) | async-done | bytes 4194320 | tf_op jit(solution)/shard_map/psum | solution.py:239
  318.3 4.6 %fusion.3 = (f32[1024]{0:T(1024)S(1)}, bf16[1024,2048]{1,0:T(8,128)(2,1)S(1)}) fusion(bf16[1024,2048]{1,0:T(8,128)(2,1)} %all-reduce.2.cloned.1.call-done, bf16[16,1024,128]{2,1,0:T(8,128)(2,1)} %gather_fusion.1, pred[16]{0:T(512)(128)(4,1)S(1)} %get-tuple-element.8), kind=kLoop, calls=%fused_computation.10 | loop fusion | flops 16776192 | bytes 12587024 | tf_op jit(solution)/shard_map/reduce_sum | solution.py:19
  323.0 6.3 %fusion.10 = f32[1024,1024]{1,0:T(8,128)} fusion(bf16[2048,1024]{1,0:T(8,128)(2,1)S(1)} %copy-done.4, bf16[1024,2048]{1,0:T(8,128)(2,1)S(1)} %get-tuple-element.5, f32[2048]{0:T(1024)S(1)} %convert_element_type.97, f32[1024]{0:T(1024)S(1)} %add_rsqrt_fusion), kind=kOutput, calls=%fused_computation.28 | convolution fusion | flops 4303355904 | bytes 12595200 | tf_op jit(solution)/shard_map/dot_general | solution.py:245
  329.3 15.4 %convolution_convert_fusion.1 = bf16[1024,2048]{1,0:T(8,128)(2,1)} fusion(bf16[1024,2048]{0,1:T(8,128)(2,1)} %bitcast.88, f32[1024,1024]{1,0:T(8,128)} %fusion.10, bf16[2048,1024]{1,0:T(8,128)(2,1)} %reshape_reshape.7, bf16[1024,2048]{1,0:T(8,128)(2,1)} %copy-done.3, f32[2048]{0:T(1024)S(1)} %convert_element_type.97, f32[1024]{0:T(1024)S(1)} %add_rsqrt_fusion), kind=kOutput, calls=%fused_computation.20 | convolution fusion | flops 8606711808 | bytes 20983808 | tf_op jit(solution)/shard_map/dot_general | solution.py:254
  344.7 38.1 %reduce-scatter.2.cloned.1.call-done = bf16[1024,256]{1,0:T(8,128)(2,1)} async-done(((bf16[1024,2048]{1,0:T(8,128)(2,1)}), bf16[1024,256]{1,0:T(8,128)(2,1)}) %reduce-scatter.2.cloned.1.call-update) | async-done | bytes 524304 | tf_op jit(solution)/shard_map/reduce_scatter | solution.py:257
  382.8 2.1 add_convert_fusion
  (47 shorter events, 1.0 us)
Async XLA Ops:
  7.2 15.2 %copy-start = (bf16[2048]{0:T(1024)(128)(2,1)S(1)}, bf16[2048]{0:T(1024)(128)(2,1)}, u32[]{:S(2)}) copy-start(bf16[2048]{0:T(1024)(128)(2,1)} %param.16) | copy-start | bytes 12292
  7.2 10.1 %copy-start.8 = (bf16[3,128,256]{2,1,0:T(8,128)(2,1)S(1)}, bf16[3,128,256]{2,1,0:T(8,128)(2,1)}, u32[]{:S(2)}) copy-start(bf16[3,128,256]{2,1,0:T(8,128)(2,1)} %param.14) | copy-start | bytes 589828
  7.2 216.5 %all-gather.3.cloned.1.call-start = ((), (), s32[]{:S(2)}) async-start(), calls=%async_computation.3 | async-start | bytes 14483456 | tf_op jit(solution)/shard_map/all_gather | solution.py:45
  11.4 306.9 %all-reduce.2.cloned.1.call-start = ((), (), s32[]{:S(2)}) async-start(), calls=%async_computation.1 | async-start | bytes 8388608 | tf_op jit(solution)/shard_map/psum | solution.py:239
  12.7 25.3 %collective-permute-start.1 = (bf16[1024,256]{0,1:T(8,128)(2,1)S(1)}, bf16[1024,256]{0,1:T(8,128)(2,1)S(1)}, u32[]{:S(2)}, u32[]{:S(2)}) collective-permute-start(bf16[1024,256]{0,1:T(8,128)(2,1)S(1)} %copy.19), channel_id=1, source_target_pairs={{0,6},{1,7},{2,0},{3,1},{4,2},{5,3},{6,4},{7,5},{8,14},{9,15},{10,... | collective-permute-start | bytes 1572872 | tf_op jit(solution)/shard_map/ppermute | solution.py:177
  15.6 26.3 %collective-permute-start.2 = (bf16[1024,256]{0,1:T(8,128)(2,1)S(1)}, bf16[1024,256]{0,1:T(8,128)(2,1)S(1)}, u32[]{:S(2)}, u32[]{:S(2)}) collective-permute-start(bf16[1024,256]{0,1:T(8,128)(2,1)S(1)} %copy.19), channel_id=1, source_target_pairs={{0,4},{1,5},{2,6},{3,7},{4,0},{5,1},{6,2},{7,3},{8,12},{9,13},{10,... | collective-permute-start | bytes 1572872 | tf_op jit(solution)/shard_map/ppermute | solution.py:177
  16.4 26.6 %collective-permute-start.3 = (bf16[1024,256]{0,1:T(8,128)(2,1)S(1)}, bf16[1024,256]{0,1:T(8,128)(2,1)S(1)}, u32[]{:S(2)}, u32[]{:S(2)}) collective-permute-start(bf16[1024,256]{0,1:T(8,128)(2,1)S(1)} %copy.19), channel_id=1, source_target_pairs={{0,2},{1,3},{2,4},{3,5},{4,6},{5,7},{6,0},{7,1},{8,10},{9,11},{10,... | collective-permute-start | bytes 1572872 | tf_op jit(solution)/shard_map/ppermute | solution.py:177
  17.3 40.3 %collective-permute-start = (bf16[1024,256]{0,1:T(8,128)(2,1)S(1)}, bf16[1024,256]{0,1:T(8,128)(2,1)}, u32[]{:S(2)}, u32[]{:S(2)}) collective-permute-start(bf16[1024,256]{0,1:T(8,128)(2,1)S(1)} %copy.19), channel_id=1, source_target_pairs={{0,1},{1,0},{2,3},{3,2},{4,5},{5,4},{6,7},{7,6},{8,9},{9,8},{10,11... | collective-permute-start | bytes 1572872 | tf_op jit(solution)/shard_map/ppermute | solution.py:180
  17.3 27.1 %collective-permute-start.5 = (bf16[3,128,256]{2,1,0:T(8,128)(2,1)S(1)}, bf16[3,128,256]{2,1,0:T(8,128)(2,1)S(1)}, u32[]{:S(2)}, u32[]{:S(2)}) collective-permute-start(bf16[3,128,256]{2,1,0:T(8,128)(2,1)S(1)} %copy-done.8), channel_id=1, source_target_pairs={{0,24},{8,0},{16,8},{24,16},{32,56},{40,32},{48,40},{56,48},{64,88... | collective-permute-start | bytes 589832 | tf_op jit(solution)/shard_map/ppermute | solution.py:35
  38.0 11.0 %collective-permute-start.6 = (bf16[3,128,256]{2,1,0:T(8,128)(2,1)S(1)}, bf16[3,128,256]{2,1,0:T(8,128)(2,1)S(1)}, u32[]{:S(2)}, u32[]{:S(2)}) collective-permute-start(bf16[3,128,256]{2,1,0:T(8,128)(2,1)S(1)} %copy-done.8), channel_id=1, source_target_pairs={{0,16},{8,24},{16,0},{24,8},{32,48},{40,56},{48,32},{56,40},{64,80... | collective-permute-start | bytes 589832 | tf_op jit(solution)/shard_map/ppermute | solution.py:35
  41.9 9.0 %collective-permute-start.7 = (bf16[3,128,256]{2,1,0:T(8,128)(2,1)S(1)}, bf16[3,128,256]{2,1,0:T(8,128)(2,1)S(1)}, u32[]{:S(2)}, u32[]{:S(2)}) collective-permute-start(bf16[3,128,256]{2,1,0:T(8,128)(2,1)S(1)} %copy-done.8), channel_id=1, source_target_pairs={{0,8},{8,16},{16,24},{24,0},{32,40},{40,48},{48,56},{56,32},{64,72... | collective-permute-start | bytes 589832 | tf_op jit(solution)/shard_map/ppermute | solution.py:35
  44.3 83.0 %collective-permute-start.4 = (bf16[3,1024,256]{1,2,0:T(8,128)(2,1)}, bf16[3,1024,256]{1,2,0:T(8,128)(2,1)}, u32[]{:S(2)}, u32[]{:S(2)}) collective-permute-start(bf16[3,1024,256]{1,2,0:T(8,128)(2,1)} %pad_maximum_fusion.1), channel_id=1, source_target_pairs={{0,1},{1,0},{2,3},{3,2},{4,5},{5,4},{6,7},{7,6},{8,9},{9,8},{10,11... | collective-permute-start | bytes 4718600 | tf_op jit(solution)/shard_map/ppermute | solution.py:181
  52.3 39.2 %collective-permute-start.8 = (bf16[3,4,128,256]{3,2,0,1:T(8,128)(2,1)}, bf16[3,4,128,256]{3,2,0,1:T(8,128)(2,1)S(1)}, u32[]{:S(2)}, u32[]{:S(2)}) collective-permute-start(bf16[3,4,128,256]{3,2,0,1:T(8,128)(2,1)} %get-tuple-element.19), channel_id=1, source_target_pairs={{0,96},{8,104},{16,112},{24,120},{32,0},{40,8},{48,16},{56,24},{64... | collective-permute-start | bytes 2359304 | tf_op jit(solution)/shard_map/ppermute | solution.py:37
  55.0 37.1 %collective-permute-start.9 = (bf16[3,4,128,256]{3,2,0,1:T(8,128)(2,1)}, bf16[3,4,128,256]{3,2,0,1:T(8,128)(2,1)}, u32[]{:S(2)}, u32[]{:S(2)}) collective-permute-start(bf16[3,4,128,256]{3,2,0,1:T(8,128)(2,1)} %get-tuple-element.19), channel_id=1, source_target_pairs={{0,64},{8,72},{16,80},{24,88},{32,96},{40,104},{48,112},{56,120},{... | collective-permute-start | bytes 2359304 | tf_op jit(solution)/shard_map/ppermute | solution.py:37
  55.8 60.2 %collective-permute-start.10 = (bf16[3,4,128,256]{3,2,0,1:T(8,128)(2,1)}, bf16[3,4,128,256]{3,2,0,1:T(8,128)(2,1)}, u32[]{:S(2)}, u32[]{:S(2)}) collective-permute-start(bf16[3,4,128,256]{3,2,0,1:T(8,128)(2,1)} %get-tuple-element.19), channel_id=1, source_target_pairs={{0,32},{8,40},{16,48},{24,56},{32,64},{40,72},{48,80},{56,88},{64,... | collective-permute-start | bytes 2359304 | tf_op jit(solution)/shard_map/ppermute | solution.py:37
  91.4 24.6 %copy-start.7 = (bf16[3,4,128,256]{3,2,0,1:T(8,128)(2,1)}, bf16[3,4,128,256]{3,2,0,1:T(8,128)(2,1)S(1)}, u32[]{:S(2)}) copy-start(bf16[3,4,128,256]{3,2,0,1:T(8,128)(2,1)S(1)} %collective-permute-done.8) | copy-start | bytes 2359300
  136.0 7.6 %copy-start.5 = (bf16[1024,2,128]{2,0,1:T(8,128)(2,1)S(1)}, bf16[1024,2,128]{2,0,1:T(8,128)(2,1)}, u32[]{:S(2)}) copy-start(bf16[1024,2,128]{2,0,1:T(8,128)(2,1)} %copy.31) | copy-start | bytes 1572868
  149.7 3.6 copy-start.2
  223.7 1.9 copy-start.6
  228.9 0.7 copy-start.9
  228.9 153.9 %reduce-scatter.2.cloned.1.call-start = ((), (), s32[]{:S(2)}) async-start(), calls=%async_computation.2 | async-start | bytes 4718592 | tf_op jit(solution)/shard_map/reduce_scatter | solution.py:257
  318.3 4.7 %copy-start.4 = (bf16[2048,1024]{1,0:T(8,128)(2,1)S(1)}, bf16[2048,1024]{1,0:T(8,128)(2,1)}, u32[]{:S(2)}) copy-start(bf16[2048,1024]{1,0:T(8,128)(2,1)} %reshape_reshape.6) | copy-start | bytes 12582916
  322.9 6.3 %copy-start.3 = (bf16[1024,2048]{1,0:T(8,128)(2,1)}, bf16[1024,2048]{1,0:T(8,128)(2,1)S(1)}, u32[]{:S(2)}) copy-start(bf16[1024,2048]{1,0:T(8,128)(2,1)S(1)} %get-tuple-element.5) | copy-start | bytes 12582916
  329.3 55.7 %copy-start.1 = (bf16[2048]{0:T(1024)(128)(2,1)S(1)}, bf16[2048]{0:T(1024)(128)(2,1)}, u32[]{:S(2)}) copy-start(bf16[2048]{0:T(1024)(128)(2,1)} %param.16) | copy-start | bytes 12292
Sparse Core Ops, SparseCore 0:
  11.5 130.6 all-gather.2
  229.1 89.1 all-reduce.1
  344.8 37.9 reduce-scatter.1

commit v4 on v1

--- a/solution.py
+++ b/solution.py
@@ -162,9 +162,9 @@
     qkv_shifted, row, col = gather_req_shifted(w_qkv, 1, "req")
     side = qkv_shifted.shape[1]
     w_qkv_full = qkv_shifted.reshape(3, -1, w_qkv.shape[2])
-    w_gate_full, w_up_full, w_down_full, w_out_full = gather_packed(
-        [w_gate, w_up, w_down, w_out], [0, 0, 1, 1], "req"
-    )
+    out_shifted, _, _ = gather_req_shifted(w_out, 1, "req")
+    w_out_full = jnp.roll(out_shifted, (row, col), axis=(1, 2)).reshape(w_out.shape[0], -1)
+    w_gate_full, w_up_full, w_down_full = gather_packed([w_gate, w_up, w_down], [0, 0, 1], "req")
     width = w_qkv.shape[2]
     heads_local = width // HD
     slots = k_cache.shape[1]
@@ -211,7 +211,8 @@
     partial_value = jnp.dot(
         attn, w_out_full, preferred_element_type=jnp.float32
     )
-    summed = lax.psum(partial_value.astype(jnp.bfloat16), "mp").astype(jnp.float32)
+    after_pack = (w_gate_full[0, 0] * 0).astype(jnp.bfloat16)
+    summed = lax.psum(partial_value.astype(jnp.bfloat16) + after_pack, "mp").astype(jnp.float32)
     mid_full = (full_rows.astype(jnp.float32) + summed).astype(jnp.bfloat16)
     own = hidden_in.shape[1]
     mid_local = lax.dynamic_slice_in_dim(mid_full, lax.axis_index("mp") * own, own, axis=1)

time: 300 us -> 327 us (1.090); the launches traced: 299 us -> 322 us
  waiting for transfers between devices: 127 us -> 149 us
  Pallas kernels: 41.9 us -> 25.8 us
  starting transfers between devices: 10.3 us -> 25 us
    ppermute x3 -> x6, waiting for transfers between devices: 1.45 us -> 27.4 us  [gather_req_shifted(): lax.ppermute(stage, axis_name, outer(k))]
    psum x1, waiting for transfers between devices: 41.3 us -> 60.2 us  [on_device(): lax.psum(partial_value.astype(jnp.bfloat16) + after_pack, 'mp')]
    pallas_call x1, Pallas kernels: 41.9 us -> 25.8 us  [flash_attention(): pl.pallas_call(body, grid_spec=grid_spec, out_shape=jax.ShapeDtypeStruct(...]
    all_gather x1, waiting for transfers between devices: 15.1 us -> 0.02 us  [on_device(): full_rows = lax.all_gather(hidden_in, 'mp', axis=1, tiled=True)]
    ppermute x3 -> x6, starting transfers between devices: 4.68 us -> 12.6 us  [gather_req_shifted(): lax.ppermute(stage, axis_name, outer(k))]
    ppermute x3 -> x6, starting transfers between devices: 5.45 us -> 12.3 us  [gather_req_shifted(): lax.ppermute(block, axis_name, inner(k))]
    ppermute x3 -> x6, waiting for transfers between devices: 9.82 us -> 4.26 us  [gather_req_shifted(): lax.ppermute(block, axis_name, inner(k))]
    transpose x3 -> x1, local copies, waits for them, and re-layouts: 8.26 us -> 6.45 us  [gather_packed(): piece = jnp.moveaxis(piece, 0, axis)]
  transfers between devices with their start and end apart: 10 -> 16, of which waited for: 8 -> 7; matrix products, arithmetic and copies ran while one was open for 23% -> 17% of each run, Pallas kernels for 14% -> 8%
where the time goes in v4:
time: 327 us; the launch traced here: 322 us
  waiting for transfers between devices  149 us (46%)
  local copies, waits for them, and re-layouts  49.3 us (15%)
  matrix products  31.7 us (10%)
  Pallas kernels  25.8 us (8%)
  other arithmetic  25.3 us (8%)
  starting transfers between devices  25 us (8%)
  between operations  15.8 us (5%)
    psum x1, waiting for transfers between devices, on_device(): lax.psum(partial_value.astype(jnp.bfloat16) + after_pack, 'mp')  60.2 us
    reduce_scatter x1, waiting for transfers between devices, on_device(): lax.psum_scatter(terms.astype(jnp.bfloat16), 'mp', scatter_dimension=1, t...  38.1 us
    ppermute x6, waiting for transfers between devices, gather_req_shifted(): lax.ppermute(stage, axis_name, outer(k))  27.4 us
    pallas_call x1, Pallas kernels, flash_attention(): pl.pallas_call(body, grid_spec=grid_spec, out_shape=jax.ShapeDtypeStruct(...  25.8 us
    all_gather x1, waiting for transfers between devices, gather_packed(): gathered = lax.all_gather(joined, axis_name, axis=0, tiled=False)  18.6 us
    dot_general x1, matrix products, on_device(): terms = jnp.dot(units, w_down_full, preferred_element_type=jnp.float32)  15.3 us
    another operation x2, local copies, waits for them, and re-layouts, gather_packed(): outs.append(piece.reshape(shape))  14.7 us
    ppermute x6, starting transfers between devices, gather_req_shifted(): lax.ppermute(stage, axis_name, outer(k))  12.6 us
  transfers between devices with their start and end apart: 16, of which 7 were waited for; matrix products, arithmetic and copies ran while one was open for 17% of the time, Pallas kernels for 8%

profile of v4, /device:TPU:0, one launch (start us, length us, event | category | flops | bytes accessed | tf_op | source)
XLA Modules:
  0.0 322.2 jit_solution(15652703124722038011)
XLA Ops:
  7.2 0.0 all-gather.4.cloned.1.call-start
  7.2 0.7 all-gather.4.cloned.1.call-update
  7.9 0.0 all-gather.6.cloned.1.call-start
  8.0 1.1 reshape.98
  9.0 1.1 reshape.97
  10.1 2.0 pad_maximum_fusion.1
  12.1 0.0 all-gather.6.cloned.1.call-update
  12.1 0.0 all-reduce.2.cloned.1.call-start
  12.2 1.1 copy.37
  13.3 2.1 collective-permute-start.2
  15.3 3.6 %collective-permute-start.1 = (bf16[3,128,256]{1,2,0:T(8,128)(2,1)S(1)}, bf16[3,128,256]{1,2,0:T(8,128)(2,1)S(1)}, u32[]{:S(2)}, u32[]{:S(2)}) collective-permute-start(bf16[3,128,256]{1,2,0:T(8,128)(2,1)S(1)} %copy.37), channel_id=1, source_target_pairs={{0,16},{8,24},{16,0},{24,8},{32,48},{40,56},{48,32},{56,40},{64,80... | collective-permute-start | bytes 589832 | tf_op jit(solution)/shard_map/ppermute | solution.py:35
  18.9 0.1 copy.45
  19.0 0.1 collective-permute-start.8
  19.1 2.5 collective-permute-start.7
  21.6 0.8 collective-permute-start.6
  23.0 4.1 %collective-permute-done.8 = bf16[256,128]{0,1:T(8,128)(2,1)S(1)} collective-permute-done((bf16[256,128]{0,1:T(8,128)(2,1)S(1)}, bf16[256,128]{0,1:T(8,128)(2,1)S(1)}, u32[]{:S(2)}, u32[]{:S(2)}) %collective-permute-start.8) | collective-permute-done | bytes 65568 | tf_op jit(solution)/shard_map/ppermute | solution.py:35
  27.1 3.3 %collective-permute-start = (bf16[3,128,256]{1,2,0:T(8,128)(2,1)S(1)}, bf16[3,128,256]{1,2,0:T(8,128)(2,1)S(1)}, u32[]{:S(2)}, u32[]{:S(2)}) collective-permute-start(bf16[3,128,256]{1,2,0:T(8,128)(2,1)S(1)} %copy.37), channel_id=1, source_target_pairs={{0,24},{8,0},{16,8},{24,16},{32,56},{40,32},{48,40},{56,48},{64,88... | collective-permute-start | bytes 589832 | tf_op jit(solution)/shard_map/ppermute | solution.py:35
  30.5 0.1 collective-permute-done.7
  30.6 0.0 collective-permute-done.6
  30.6 3.1 collective-permute-start.9
  33.8 0.7 collective-permute-start.10
  34.5 0.0 collective-permute-done.2
  34.5 1.0 collective-permute-start.11
  35.5 0.0 collective-permute-done.1
  35.5 0.0 collective-permute-done
  35.5 0.1 fusion.54
  35.7 2.0 collective-permute-start.5
  37.6 1.8 collective-permute-start.4
  39.5 22.4 %collective-permute-done.9 = bf16[256,4,128]{0,2,1:T(8,128)(2,1)S(1)} collective-permute-done((bf16[256,4,128]{0,2,1:T(8,128)(2,1)S(1)}, bf16[256,4,128]{0,2,1:T(8,128)(2,1)S(1)}, u32[]{:S(2)}, u32[]{:S(2)}) %collective-permute-start.9) | collective-permute-done | bytes 262176 | tf_op jit(solution)/shard_map/ppermute | solution.py:37
  61.8 4.0 %collective-permute-start.3 = (bf16[3,4,128,256]{2,3,1,0:T(8,128)(2,1)S(1)}, bf16[3,4,128,256]{2,3,1,0:T(8,128)(2,1)}, u32[]{:S(2)}, u32[]{:S(2)}) collective-permute-start(bf16[3,4,128,256]{2,3,1,0:T(8,128)(2,1)S(1)} %get-tuple-element.11), channel_id=1, source_target_pairs={{0,96},{8,104},{16,112},{24,120},{32,0},{40,8},{48,16},{56,24},{64... | collective-permute-start | bytes 2359304 | tf_op jit(solution)/shard_map/ppermute | solution.py:37
  65.8 0.0 collective-permute-done.10
  66.0 0.1 constant_dynamic-slice_fusion
  66.1 0.4 fusion.38
  66.5 0.0 all-gather.4.cloned.1.call-done
  66.6 3.2 %fusion.3 = f32[1024]{0:T(1024)S(1)} fusion(bf16[1024,2048]{1,0:T(8,128)(2,1)} %all-gather.4.cloned.1.call-done), kind=kLoop, calls=%fused_computation.8 | loop fusion | flops 6290432 | bytes 4198400 | tf_op jit(solution)/shard_map/reduce_sum | solution.py:19
  69.8 0.3 copy-done
  70.1 3.0 fusion.5
  73.1 6.4 %copy.41 = bf16[1024,2048]{0,1:T(8,128)(2,1)} copy(bf16[1024,2048]{1,0:T(8,128)(2,1)} %fusion.5) | data formatting | bytes 8388608 | tf_op jit(solution)/shard_map/convert_element_type | solution.py:20
  79.5 6.3 %copy.42 = bf16[1024,4,4,128]{3,0,2,1:T(8,128)(2,1)} copy(bf16[1024,4,4,128]{0,3,2,1:T(8,128)(2,1)} %bitcast.74) | data formatting | bytes 8388608 | tf_op jit(solution)/shard_map/reshape | solution.py:173
  85.9 3.1 fusion.11
  89.0 0.0 collective-permute-done.5
  89.0 5.1 %collective-permute-done.4 = bf16[3,4,128,256]{2,3,1,0:T(8,128)(2,1)} collective-permute-done((bf16[3,4,128,256]{2,3,1,0:T(8,128)(2,1)S(1)}, bf16[3,4,128,256]{2,3,1,0:T(8,128)(2,1)}, u32[]{:S(2)}, u32[]{:S(2)}) %collective-permute-start.4) | collective-permute-done | bytes 786464 | tf_op jit(solution)/shard_map/ppermute | solution.py:37
  94.1 5.6 %fusion.19 = f32[3,1024,256]{2,1,0:T(8,128)S(1)} fusion(s32[]{:T(128)S(6)} %select_n.105, bf16[1024,4,4,128]{3,0,2,1:T(8,128)(2,1)S(1)} %fusion.11, bf16[3,1,4,128,256]{3,4,2,0,1:T(8,128)(2,1)} %bitcast.7, bf16[3,1,4,128,256]{3,4,2,0,1:T(8,128)(2,1)} %bitcast.6, bf16[3,1,4,128,256]{3,4,2,0,1:T(8,128)(2,1)} %bitcast.5, ...), kind=kOutput, calls=%fused_computation.33 | convolution fusion | flops 3228041216 | bytes 10485764 | tf_op jit(solution)/shard_map/nd,kdw->knw/dot_general | solution.py:175
  99.7 0.8 fusion.39.vn_ref
  100.5 1.2 fusion.41
  101.7 5.6 %fusion.34 = (bf16[1024,256]{1,0:T(8,128)(2,1)}, bf16[1024,256]{1,0:T(8,128)(2,1)}) fusion(f32[2,1024,256]{2,1,0:T(8,128)S(1)} %fusion.41, f32[3,1024,256]{2,1,0:T(8,128)S(1)} %fusion.19, f32[256]{0:T(256)S(1)} %get-tuple-element.12, f32[256]{0:T(256)S(1)} %get-tuple-element.13, f32[1024]{0:T(1024)S(1)} %add_convert_fusion.1), kind=kLoop, calls=%fused_computation.42 | loop fusion | flops 2621440 | bytes 5249024 | tf_op jit(solution)/shard_map/convert_element_type | solution.py:199
  107.3 25.8 %shard_map.130 = bf16[1024,256]{1,0:T(8,128)(2,1)} custom-call(s32[1]{0:T(128)} %copy.61.len_ref, bf16[1024,256]{1,0:T(8,128)(2,1)} %get-tuple-element.9.q_ref, bf16[4096,256]{1,0:T(8,128)(2,1)} %bitcast.94, bf16[4096,256]{1,0:T(8,128)(2,1)} %bitcast.95, bf16[1024,256]{1,0:T(8,128)(2,1)} %get-tuple-element.8.kn_ref, bf16[1024,256]{1,0:T(8,128)(2,1)} %fusion.39.vn_ref), custom_call_target="tpu_custom_call" | custom-call | flops 5368709120 | bytes 6291456 | tf_op jit(solution)/shard_map/pallas_call | solution.py:147
  133.1 18.6 %all-gather.6.cloned.1.call-done = bf16[49152,128]{1,0:T(8,128)(2,1)} async-done(((bf16[3072,128]{1,0:T(8,128)(2,1)}), bf16[49152,128]{1,0:T(8,128)(2,1)}) %all-gather.6.cloned.1.call-update) | async-done | bytes 12582928 | tf_op jit(solution)/shard_map/all_gather | solution.py:45
  151.6 9.0 %fusion.56 = (bf16[16,1024,128]{2,1,0:T(8,128)(2,1)}, bf16[1024,16,128]{2,0,1:T(8,128)(2,1)}, bf16[16,1024,128]{2,1,0:T(8,128)(2,1)}) fusion(bf16[16,3072,128]{2,1,0:T(8,128)(2,1)} %bitcast.75), kind=kLoop, calls=%fused_computation.92 | loop fusion | bytes 25165824 | tf_op jit(solution)/shard_map/slice | solution.py:50
  160.7 7.3 %reshape_reshape.6 = bf16[2048,1024]{1,0:T(8,128)(2,1)} reshape(bf16[16,1024,128]{2,1,0:T(8,128)(2,1)} %get-tuple-element.7) | data formatting | bytes 8388608 | tf_op jit(solution)/shard_map/reshape;reshape | solution.py:54
  168.0 1.2 slice.47
  169.8 3.2 %convert_add_fusion.1 = bf16[1024,2048]{1,0:T(8,128)(2,1)} fusion(bf16[1024,256]{1,0:T(8,128)(2,1)S(1)} %copy-done.6, bf16[256,2048]{0,1:T(8,128)(2,1)S(1)} %bitcast.77, bf16[]{:T(256)} %bitcast.33), kind=kOutput, calls=%fused_computation.22 | convolution fusion | flops 1077936128 | bytes 5767170 | tf_op jit(solution)/shard_map/dot_general | solution.py:211
  173.1 0.0 all-reduce.2.cloned.1.call-update
  173.1 0.0 reduce-scatter.2.cloned.1.call-start
  173.1 0.6 copy-done.5
  173.7 6.4 %copy.49 = bf16[1024,16,128]{0,2,1:T(8,128)(2,1)} copy(bf16[1024,16,128]{2,0,1:T(8,128)(2,1)} %get-tuple-element.6) | data formatting | bytes 8388608 | tf_op jit(solution)/shard_map/transpose | solution.py:51
  180.2 7.3 %reshape_reshape.7 = bf16[2048,1024]{1,0:T(8,128)(2,1)} reshape(bf16[16,1024,128]{2,1,0:T(8,128)(2,1)} %get-tuple-element.5) | data formatting | bytes 8388608 | tf_op jit(solution)/shard_map/reshape;reshape | solution.py:54
  187.5 60.2 %all-reduce.2.cloned.1.call-done = bf16[1024,2048]{1,0:T(8,128)(2,1)} async-done(((bf16[1024,2048]{1,0:T(8,128)(2,1)}), bf16[1024,2048]{1,0:T(8,128)(2,1)}) %all-reduce.2.cloned.1.call-update) | async-done | bytes 4194320 | tf_op jit(solution)/shard_map/psum | solution.py:215
  247.7 5.6 %fusion = (f32[1024]{0:T(1024)S(1)}, bf16[1024,2048]{1,0:T(8,128)(2,1)S(1)}) fusion(bf16[1024,2048]{1,0:T(8,128)(2,1)} %all-reduce.2.cloned.1.call-done, bf16[1024,2048]{1,0:T(8,128)(2,1)} %all-gather.4.cloned.1.call-done), kind=kLoop, calls=%fused_computation.5 | loop fusion | flops 14679040 | bytes 12587008 | tf_op jit(solution)/shard_map/reduce_sum | solution.py:19
  253.3 6.3 %fusion.27 = f32[1024,1024]{1,0:T(8,128)} fusion(bf16[2048,1024]{1,0:T(8,128)(2,1)S(1)} %copy-done.2, bf16[1024,2048]{1,0:T(8,128)(2,1)S(1)} %get-tuple-element.4, f32[2048]{0:T(1024)S(1)} %convert_element_type.80, f32[1024]{0:T(1024)S(1)} %add_rsqrt_fusion), kind=kOutput, calls=%fused_computation.38 | convolution fusion | flops 4303355904 | bytes 12595200 | tf_op jit(solution)/shard_map/dot_general | solution.py:221
  259.6 15.3 %convolution_convert_fusion = bf16[1024,2048]{1,0:T(8,128)(2,1)} fusion(bf16[1024,2048]{0,1:T(8,128)(2,1)} %bitcast.76, f32[1024,1024]{1,0:T(8,128)} %fusion.27, bf16[2048,1024]{1,0:T(8,128)(2,1)} %reshape_reshape.7, bf16[1024,2048]{1,0:T(8,128)(2,1)} %copy-done.1, f32[2048]{0:T(1024)S(1)} %convert_element_type.80, f32[1024]{0:T(1024)S(1)} %add_rsqrt_fusion), kind=kOutput, calls=%fused_computation.23 | convolution fusion | flops 8606711808 | bytes 20983808 | tf_op jit(solution)/shard_map/dot_general | solution.py:230
  275.0 0.0 reduce-scatter.2.cloned.1.call-update
  275.0 38.1 %reduce-scatter.2.cloned.1.call-done = bf16[1024,256]{1,0:T(8,128)(2,1)} async-done(((bf16[1024,2048]{1,0:T(8,128)(2,1)}), bf16[1024,256]{1,0:T(8,128)(2,1)}) %reduce-scatter.2.cloned.1.call-update) | async-done | bytes 524304 | tf_op jit(solution)/shard_map/reduce_scatter | solution.py:233
  313.1 2.1 add_convert_fusion
  (30 shorter events, 0.3 us)
Async XLA Ops:
  7.2 11.7 %copy-start.3 = (bf16[256,128]{1,0:T(8,128)(2,1)S(1)}, bf16[256,128]{1,0:T(8,128)(2,1)}, u32[]{:S(2)}) copy-start(bf16[256,128]{1,0:T(8,128)(2,1)} %param.13) | copy-start | bytes 196612
  7.2 26.6 %copy-start.4 = (bf16[2048]{0:T(1024)(128)(2,1)S(1)}, bf16[2048]{0:T(1024)(128)(2,1)}, u32[]{:S(2)}) copy-start(bf16[2048]{0:T(1024)(128)(2,1)} %param.14) | copy-start | bytes 12292
  7.2 59.4 %all-gather.4.cloned.1.call-start = ((), (), s32[]{:S(2)}) async-start(), calls=%async_computation.1 | async-start | bytes 4718592 | tf_op jit(solution)/shard_map/all_gather | solution.py:171
  7.9 143.7 %all-gather.6.cloned.1.call-start = ((), (), s32[]{:S(2)}) async-start(), calls=%async_computation.4 | async-start | bytes 13369344 | tf_op jit(solution)/shard_map/all_gather | solution.py:45
  12.1 235.6 %all-reduce.2.cloned.1.call-start = ((), (), s32[]{:S(2)}) async-start(), calls=%async_computation.2 | async-start | bytes 8388608 | tf_op jit(solution)/shard_map/psum | solution.py:215
  13.3 21.2 %collective-permute-start.2 = (bf16[3,128,256]{1,2,0:T(8,128)(2,1)S(1)}, bf16[3,128,256]{1,2,0:T(8,128)(2,1)S(1)}, u32[]{:S(2)}, u32[]{:S(2)}) collective-permute-start(bf16[3,128,256]{1,2,0:T(8,128)(2,1)S(1)} %copy.37), channel_id=1, source_target_pairs={{0,8},{8,16},{16,24},{24,0},{32,40},{40,48},{48,56},{56,32},{64,72... | collective-permute-start | bytes 589832 | tf_op jit(solution)/shard_map/ppermute | solution.py:35
  15.3 20.2 %collective-permute-start.1 = (bf16[3,128,256]{1,2,0:T(8,128)(2,1)S(1)}, bf16[3,128,256]{1,2,0:T(8,128)(2,1)S(1)}, u32[]{:S(2)}, u32[]{:S(2)}) collective-permute-start(bf16[3,128,256]{1,2,0:T(8,128)(2,1)S(1)} %copy.37), channel_id=1, source_target_pairs={{0,16},{8,24},{16,0},{24,8},{32,48},{40,56},{48,32},{56,40},{64,80... | collective-permute-start | bytes 589832 | tf_op jit(solution)/shard_map/ppermute | solution.py:35
  19.0 8.1 %collective-permute-start.8 = (bf16[256,128]{0,1:T(8,128)(2,1)S(1)}, bf16[256,128]{0,1:T(8,128)(2,1)S(1)}, u32[]{:S(2)}, u32[]{:S(2)}) collective-permute-start(bf16[256,128]{0,1:T(8,128)(2,1)S(1)} %copy.45), channel_id=1, source_target_pairs={{0,8},{8,16},{16,24},{24,0},{32,40},{40,48},{48,56},{56,32},{64,72... | collective-permute-start | bytes 196616 | tf_op jit(solution)/shard_map/ppermute | solution.py:35
  19.1 11.5 %collective-permute-start.7 = (bf16[256,128]{0,1:T(8,128)(2,1)S(1)}, bf16[256,128]{0,1:T(8,128)(2,1)S(1)}, u32[]{:S(2)}, u32[]{:S(2)}) collective-permute-start(bf16[256,128]{0,1:T(8,128)(2,1)S(1)} %copy.45), channel_id=1, source_target_pairs={{0,16},{8,24},{16,0},{24,8},{32,48},{40,56},{48,32},{56,40},{64,80... | collective-permute-start | bytes 196616 | tf_op jit(solution)/shard_map/ppermute | solution.py:35
  21.6 9.0 %collective-permute-start.6 = (bf16[256,128]{0,1:T(8,128)(2,1)S(1)}, bf16[256,128]{0,1:T(8,128)(2,1)S(1)}, u32[]{:S(2)}, u32[]{:S(2)}) collective-permute-start(bf16[256,128]{0,1:T(8,128)(2,1)S(1)} %copy.45), channel_id=1, source_target_pairs={{0,24},{8,0},{16,8},{24,16},{32,56},{40,32},{48,40},{56,48},{64,88... | collective-permute-start | bytes 196616 | tf_op jit(solution)/shard_map/ppermute | solution.py:35
  27.1 8.4 %collective-permute-start = (bf16[3,128,256]{1,2,0:T(8,128)(2,1)S(1)}, bf16[3,128,256]{1,2,0:T(8,128)(2,1)S(1)}, u32[]{:S(2)}, u32[]{:S(2)}) collective-permute-start(bf16[3,128,256]{1,2,0:T(8,128)(2,1)S(1)} %copy.37), channel_id=1, source_target_pairs={{0,24},{8,0},{16,8},{24,16},{32,56},{40,32},{48,40},{56,48},{64,88... | collective-permute-start | bytes 589832 | tf_op jit(solution)/shard_map/ppermute | solution.py:35
  30.6 31.2 %collective-permute-start.9 = (bf16[256,4,128]{0,2,1:T(8,128)(2,1)S(1)}, bf16[256,4,128]{0,2,1:T(8,128)(2,1)S(1)}, u32[]{:S(2)}, u32[]{:S(2)}) collective-permute-start(bf16[256,4,128]{0,2,1:T(8,128)(2,1)S(1)} %pad_maximum_fusion.2), channel_id=1, source_target_pairs={{0,96},{8,104},{16,112},{24,120},{32,0},{40,8},{48,16},{56,24},{64... | collective-permute-start | bytes 786440 | tf_op jit(solution)/shard_map/ppermute | solution.py:37
  33.8 32.1 %collective-permute-start.10 = (bf16[256,4,128]{0,2,1:T(8,128)(2,1)S(1)}, bf16[256,4,128]{0,2,1:T(8,128)(2,1)S(1)}, u32[]{:S(2)}, u32[]{:S(2)}) collective-permute-start(bf16[256,4,128]{0,2,1:T(8,128)(2,1)S(1)} %pad_maximum_fusion.2), channel_id=1, source_target_pairs={{0,64},{8,72},{16,80},{24,88},{32,96},{40,104},{48,112},{56,120},{... | collective-permute-start | bytes 786440 | tf_op jit(solution)/shard_map/ppermute | solution.py:37
  34.5 31.4 %collective-permute-start.11 = (bf16[256,4,128]{0,2,1:T(8,128)(2,1)S(1)}, bf16[256,4,128]{0,2,1:T(8,128)(2,1)S(1)}, u32[]{:S(2)}, u32[]{:S(2)}) collective-permute-start(bf16[256,4,128]{0,2,1:T(8,128)(2,1)S(1)} %pad_maximum_fusion.2), channel_id=1, source_target_pairs={{0,32},{8,40},{16,48},{24,56},{32,64},{40,72},{48,80},{56,88},{64,... | collective-permute-start | bytes 786440 | tf_op jit(solution)/shard_map/ppermute | solution.py:37
  35.7 53.3 %collective-permute-start.5 = (bf16[3,4,128,256]{2,3,1,0:T(8,128)(2,1)S(1)}, bf16[3,4,128,256]{2,3,1,0:T(8,128)(2,1)}, u32[]{:S(2)}, u32[]{:S(2)}) collective-permute-start(bf16[3,4,128,256]{2,3,1,0:T(8,128)(2,1)S(1)} %get-tuple-element.11), channel_id=1, source_target_pairs={{0,32},{8,40},{16,48},{24,56},{32,64},{40,72},{48,80},{56,88},{64,... | collective-permute-start | bytes 2359304 | tf_op jit(solution)/shard_map/ppermute | solution.py:37
  37.6 56.4 %collective-permute-start.4 = (bf16[3,4,128,256]{2,3,1,0:T(8,128)(2,1)S(1)}, bf16[3,4,128,256]{2,3,1,0:T(8,128)(2,1)}, u32[]{:S(2)}, u32[]{:S(2)}) collective-permute-start(bf16[3,4,128,256]{2,3,1,0:T(8,128)(2,1)S(1)} %get-tuple-element.11), channel_id=1, source_target_pairs={{0,64},{8,72},{16,80},{24,88},{32,96},{40,104},{48,112},{56,120},{... | collective-permute-start | bytes 2359304 | tf_op jit(solution)/shard_map/ppermute | solution.py:37
  61.8 32.2 %collective-permute-start.3 = (bf16[3,4,128,256]{2,3,1,0:T(8,128)(2,1)S(1)}, bf16[3,4,128,256]{2,3,1,0:T(8,128)(2,1)}, u32[]{:S(2)}, u32[]{:S(2)}) collective-permute-start(bf16[3,4,128,256]{2,3,1,0:T(8,128)(2,1)S(1)} %get-tuple-element.11), channel_id=1, source_target_pairs={{0,96},{8,104},{16,112},{24,120},{32,0},{40,8},{48,16},{56,24},{64... | collective-permute-start | bytes 2359304 | tf_op jit(solution)/shard_map/ppermute | solution.py:37
  66.5 3.5 %copy-start = (bf16[1024,2048]{1,0:T(8,128)(2,1)S(1)}, bf16[1024,2048]{1,0:T(8,128)(2,1)}, u32[]{:S(2)}) copy-start(bf16[1024,2048]{1,0:T(8,128)(2,1)} %all-gather.4.cloned.1.call-done) | copy-start | bytes 12582916
  160.7 9.2 %copy-start.6 = (bf16[1024,256]{1,0:T(8,128)(2,1)S(1)}, bf16[1024,256]{1,0:T(8,128)(2,1)}, u32[]{:S(2)}) copy-start(bf16[1024,256]{1,0:T(8,128)(2,1)} %shard_map.130) | copy-start | bytes 1572868
  173.1 0.7 copy-start.5
  173.1 140.0 %reduce-scatter.2.cloned.1.call-start = ((), (), s32[]{:S(2)}) async-start(), calls=%async_computation.3 | async-start | bytes 4718592 | tf_op jit(solution)/shard_map/reduce_scatter | solution.py:233
  247.7 5.6 %copy-start.2 = (bf16[2048,1024]{1,0:T(8,128)(2,1)S(1)}, bf16[2048,1024]{1,0:T(8,128)(2,1)}, u32[]{:S(2)}) copy-start(bf16[2048,1024]{1,0:T(8,128)(2,1)} %reshape_reshape.6) | copy-start | bytes 12582916
  253.3 6.3 %copy-start.1 = (bf16[1024,2048]{1,0:T(8,128)(2,1)}, bf16[1024,2048]{1,0:T(8,128)(2,1)S(1)}, u32[]{:S(2)}) copy-start(bf16[1024,2048]{1,0:T(8,128)(2,1)S(1)} %get-tuple-element.4) | copy-start | bytes 12582916
Sparse Core Ops, SparseCore 0:
  9.7 38.4 all-gather.3
  50.4 101.2 all-gather.5
  173.2 74.4 all-reduce.1
  275.1 37.9 reduce-scatter.1

commit v5 on v2

--- a/solution.py
+++ b/solution.py
@@ -217,13 +217,11 @@
     mid_local = lax.dynamic_slice_in_dim(mid_full, lax.axis_index("mp") * own, own, axis=1)
     normed2 = rms_scale(mid_full, mlp_gain)
     columns = normed2
-    gate = jnp.dot(
+    gate, upper = jnp.einsum(
+        "nd,kdf->knf",
         columns,
-        w_gate_full,
+        jnp.stack([w_gate_full, w_up_full]),
         preferred_element_type=jnp.float32,
-    )
-    upper = jnp.dot(
-        columns, w_up_full, preferred_element_type=jnp.float32
     )
     units = (jax.nn.silu(gate) * upper).astype(jnp.bfloat16)
     terms = jnp.dot(

time: 300 us -> 300 us (level)
  waiting for transfers between devices: 121 us -> 97.6 us
  local copies, waits for them, and re-layouts: 48.9 us -> 62.1 us
  Pallas kernels: 47.3 us -> 58.1 us
    another operation x2 -> x4, local copies, waits for them, and re-layouts: 14.7 us -> 27.9 us  [on_device(): jnp.stack([w_gate_full, w_up_full])]
    psum x1, waiting for transfers between devices: 41.3 us -> 28.4 us  [on_device(): lax.psum(partial_value.astype(jnp.bfloat16), 'mp').astype(jnp.float32)]
    pallas_call x1, Pallas kernels: 47.3 us -> 58.1 us  [flash_attention(): pl.pallas_call(body, grid_spec=grid_spec, out_shape=jax.ShapeDtypeStruct(...]
    all_gather x1, waiting for transfers between devices: 14.7 us -> 3.97 us  [gather_packed(): gathered = lax.all_gather(joined, axis_name, axis=0, tiled=False)]
    dot_general x1, matrix products: 15.4 us -> 9.88 us  [on_device(): terms = jnp.dot(units, w_down_full, preferred_element_type=jnp.float32)]
    dot_general x1, matrix products: 6.32 us -> 11.8 us  [on_device(): jnp.einsum('nd,kdf->knf', columns, jnp.stack([w_gate_full, w_up_full]), p...]
  transfers between devices with their start and end apart: 10 -> 10, of which waited for: 8 -> 8; matrix products, arithmetic and copies ran while one was open for 23% -> 28% of each run, Pallas kernels for 16% -> 19%
where the time goes in v5:
time: 300 us; the launch traced here: 299 us
  waiting for transfers between devices  97.6 us (33%)
  local copies, waits for them, and re-layouts  62.1 us (21%)
  Pallas kernels  58.1 us (19%)
  matrix products  31.6 us (11%)
  other arithmetic  24.8 us (8%)
  between operations  14.6 us (5%)
  starting transfers between devices  10.3 us (3%)
    pallas_call x1, Pallas kernels, flash_attention(): pl.pallas_call(body, grid_spec=grid_spec, out_shape=jax.ShapeDtypeStruct(...  58.1 us
    reduce_scatter x1, waiting for transfers between devices, on_device(): lax.psum_scatter(terms.astype(jnp.bfloat16), 'mp', scatter_dimension=1, t...  38.1 us
    psum x1, waiting for transfers between devices, on_device(): lax.psum(partial_value.astype(jnp.bfloat16), 'mp').astype(jnp.float32)  28.4 us
    another operation x4, local copies, waits for them, and re-layouts, on_device(): jnp.stack([w_gate_full, w_up_full])  27.9 us
    all_gather x1, waiting for transfers between devices, on_device(): full_rows = lax.all_gather(hidden_in, 'mp', axis=1, tiled=True)  15.1 us
    dot_general x1, matrix products, on_device(): jnp.einsum('nd,kdf->knf', columns, jnp.stack([w_gate_full, w_up_full]), p...  11.8 us
    dot_general x1, matrix products, on_device(): terms = jnp.dot(units, w_down_full, preferred_element_type=jnp.float32)  9.88 us
    ppermute x3, waiting for transfers between devices, gather_req_shifted(): lax.ppermute(block, axis_name, inner(k))  9.82 us
  transfers between devices with their start and end apart: 10, of which 8 were waited for; matrix products, arithmetic and copies ran while one was open for 28% of the time, Pallas kernels for 19%

profile of v5, /device:TPU:0, one launch (start us, length us, event | category | flops | bytes accessed | tf_op | source)
XLA Modules:
  0.0 299.0 jit_solution(2637819843482765233)
XLA Ops:
  7.2 0.0 copy-start.6
  7.2 0.0 copy-start.7
  7.2 0.0 all-gather.4.cloned.1.call-start
  7.2 0.7 all-gather.4.cloned.1.call-update
  7.9 0.0 all-gather.6.cloned.1.call-start
  8.0 1.1 reshape.95
  9.0 1.1 reshape.96
  10.1 1.9 pad_maximum_fusion
  12.0 0.0 all-gather.6.cloned.1.call-update
  12.1 0.0 all-reduce.2.cloned.1.call-start
  12.1 0.0 copy-done.6
  12.1 0.2 copy.37
  12.3 4.2 %collective-permute-start = (bf16[3,128,256]{1,2,0:T(8,128)(2,1)S(1)}, bf16[3,128,256]{1,2,0:T(8,128)(2,1)S(1)}, u32[]{:S(2)}, u32[]{:S(2)}) collective-permute-start(bf16[3,128,256]{1,2,0:T(8,128)(2,1)S(1)} %copy.37), channel_id=1, source_target_pairs={{0,24},{8,0},{16,8},{24,16},{32,56},{40,32},{48,40},{56,48},{64,88... | collective-permute-start | bytes 589832 | tf_op jit(solution)/shard_map/ppermute | solution.py:35
  16.5 0.0 collective-permute-start.1
  16.5 1.3 collective-permute-start.2
  17.7 0.0 copy-done.7
  18.4 6.4 %collective-permute-done = bf16[3,128,256]{1,2,0:T(8,128)(2,1)S(1)} collective-permute-done((bf16[3,128,256]{1,2,0:T(8,128)(2,1)S(1)}, bf16[3,128,256]{1,2,0:T(8,128)(2,1)S(1)}, u32[]{:S(2)}, u32[]{:S(2)}) %collective-permute-start) | collective-permute-done | bytes 196640 | tf_op jit(solution)/shard_map/ppermute | solution.py:35
  24.9 1.0 collective-permute-done.1
  25.8 2.5 collective-permute-done.2
  28.3 0.1 fusion.65
  28.4 3.1 %collective-permute-start.3 = (bf16[3,4,128,256]{2,3,1,0:T(8,128)(2,1)S(1)}, bf16[3,4,128,256]{2,3,1,0:T(8,128)(2,1)S(1)}, u32[]{:S(2)}, u32[]{:S(2)}) collective-permute-start(bf16[3,4,128,256]{2,3,1,0:T(8,128)(2,1)S(1)} %get-tuple-element.11), channel_id=1, source_target_pairs={{0,96},{8,104},{16,112},{24,120},{32,0},{40,8},{48,16},{56,24},{64... | collective-permute-start | bytes 2359304 | tf_op jit(solution)/shard_map/ppermute | solution.py:37
  31.5 0.6 collective-permute-start.4
  32.1 1.0 collective-permute-start.5
  33.1 15.1 %all-gather.4.cloned.1.call-done = bf16[1024,2048]{1,0:T(8,128)(2,1)} async-done(((bf16[1024,256]{1,0:T(8,128)(2,1)}), bf16[1024,2048]{1,0:T(8,128)(2,1)}) %all-gather.4.cloned.1.call-update) | async-done | bytes 4194320 | tf_op jit(solution)/shard_map/all_gather | solution.py:171
  48.2 3.2 %fusion.3 = f32[1024]{0:T(1024)S(1)} fusion(bf16[1024,2048]{1,0:T(8,128)(2,1)} %all-gather.4.cloned.1.call-done), kind=kLoop, calls=%fused_computation.8 | loop fusion | flops 6290432 | bytes 4198400 | tf_op jit(solution)/shard_map/reduce_sum | solution.py:19
  51.5 0.2 copy-done
  51.7 3.1 %fusion.5 = bf16[1024,2048]{1,0:T(8,128)(2,1)} fusion(bf16[1024,2048]{1,0:T(8,128)(2,1)S(1)} %copy-done, f32[2048]{0:T(1024)S(1)} %convert_element_type.71, f32[1024]{0:T(1024)S(1)} %add_rsqrt_fusion.1), kind=kLoop, calls=%fused_computation.10 | loop fusion | flops 8388608 | bytes 8400896 | tf_op jit(solution)/shard_map/convert_element_type | solution.py:20
  54.7 6.4 %copy.41 = bf16[1024,2048]{0,1:T(8,128)(2,1)} copy(bf16[1024,2048]{1,0:T(8,128)(2,1)} %fusion.5) | data formatting | bytes 8388608 | tf_op jit(solution)/shard_map/convert_element_type | solution.py:20
  61.1 6.4 %copy.42 = bf16[1024,4,4,128]{3,0,2,1:T(8,128)(2,1)} copy(bf16[1024,4,4,128]{0,3,2,1:T(8,128)(2,1)} %bitcast.67) | data formatting | bytes 8388608 | tf_op jit(solution)/shard_map/reshape | solution.py:173
  67.5 3.1 %fusion.15 = bf16[1024,4,4,128]{3,0,2,1:T(8,128)(2,1)S(1)} fusion(s32[]{:T(128)S(6)} %select_n.82, bf16[1024,4,4,128]{3,0,2,1:T(8,128)(2,1)} %copy.42), kind=kLoop, calls=%fused_computation.23 | loop fusion | flops 2097152 | bytes 8388612 | tf_op jit(solution)/shard_map/jit(_roll_dynamic)/concatenate | solution.py:174
  70.6 0.0 collective-permute-done.3
  70.6 0.0 collective-permute-done.4
  70.6 1.4 collective-permute-done.5
  72.1 5.4 %fusion.35 = f32[3,1024,256]{2,1,0:T(8,128)S(1)} fusion(s32[]{:T(128)S(6)} %select_n.85, bf16[1024,4,4,128]{3,0,2,1:T(8,128)(2,1)S(1)} %fusion.15, bf16[3,1,4,128,256]{3,4,2,0,1:T(8,128)(2,1)} %bitcast.7, bf16[3,1,4,128,256]{3,4,2,0,1:T(8,128)(2,1)} %bitcast.6, bf16[3,1,4,128,256]{3,4,2,0,1:T(8,128)(2,1)S(1)} %bitcast.78, ...), kind=kOutput, calls=%fused_computation.41 | convolution fusion | flops 3228041216 | bytes 10485764 | tf_op jit(solution)/shard_map/nd,kdw->knw/dot_general | solution.py:175
  77.5 0.8 fusion.49.vn_ref
  78.3 1.2 fusion.51
  79.5 5.6 %fusion.45 = (bf16[1024,256]{1,0:T(8,128)(2,1)}, bf16[1024,256]{1,0:T(8,128)(2,1)}) fusion(f32[2,1024,256]{2,1,0:T(8,128)S(1)} %fusion.51, f32[3,1024,256]{2,1,0:T(8,128)S(1)} %fusion.35, f32[256]{0:T(256)S(1)} %get-tuple-element.12, f32[256]{0:T(256)S(1)} %get-tuple-element.13, f32[1024]{0:T(1024)S(1)} %add_convert_fusion.1), kind=kLoop, calls=%fused_computation.49 | loop fusion | flops 2621440 | bytes 5249024 | tf_op jit(solution)/shard_map/convert_element_type | solution.py:199
  85.1 58.1 %shard_map.130 = bf16[1024,256]{1,0:T(8,128)(2,1)} custom-call(s32[1]{0:T(128)} %copy.53.len_ref, bf16[1024,256]{1,0:T(8,128)(2,1)} %get-tuple-element.9.q_ref, bf16[4096,256]{1,0:T(8,128)(2,1)} %bitcast.76, bf16[4096,256]{1,0:T(8,128)(2,1)} %bitcast.77, bf16[1024,256]{1,0:T(8,128)(2,1)} %get-tuple-element.8.kn_ref, bf16[1024,256]{1,0:T(8,128)(2,1)} %fusion.49.vn_ref), custom_call_target="tpu_custom_call" | custom-call | flops 5368709120 | bytes 6291456 | tf_op jit(solution)/shard_map/pallas_call | solution.py:147
  143.1 4.0 %all-gather.6.cloned.1.call-done = bf16[53248,128]{1,0:T(8,128)(2,1)} async-done(((bf16[3328,128]{1,0:T(8,128)(2,1)}), bf16[53248,128]{1,0:T(8,128)(2,1)}) %all-gather.6.cloned.1.call-update) | async-done | bytes 13631504 | tf_op jit(solution)/shard_map/all_gather | solution.py:45
  147.1 1.3 slice_bitcast_fusion.1
  148.4 0.5 copy.45
  148.9 0.0 copy-done.5
  148.9 3.3 %convolution_convert_fusion = bf16[1024,2048]{1,0:T(8,128)(2,1)} fusion(bf16[1024,256]{1,0:T(8,128)(2,1)S(1)} %copy-done.5, bf16[256,2048]{0,1:T(8,128)(2,1)S(1)} %bitcast.70), kind=kOutput, calls=%fused_computation.30 | convolution fusion | flops 1075838976 | bytes 5767168 | tf_op jit(solution)/shard_map/dot_general | solution.py:211
  152.3 0.0 all-reduce.2.cloned.1.call-update
  152.3 0.0 reduce-scatter.2.cloned.1.call-start
  152.4 0.6 copy-done.8
  153.0 9.1 %fusion.67 = (bf16[16,1024,128]{2,1,0:T(8,128)(2,1)}, bf16[1024,16,128]{2,0,1:T(8,128)(2,1)}, bf16[16,1024,128]{2,1,0:T(8,128)(2,1)}) fusion(bf16[16,3328,128]{2,1,0:T(8,128)(2,1)} %bitcast.69), kind=kLoop, calls=%fused_computation.90 | loop fusion | bytes 25165824 | tf_op jit(solution)/shard_map/slice | solution.py:50
  162.1 7.4 %stack_reshape_reshape.6 = bf16[1,2048,1024]{2,1,0:T(8,128)(2,1)} reshape(bf16[16,1024,128]{2,1,0:T(8,128)(2,1)} %get-tuple-element.5) | data formatting | bytes 8388608 | tf_op jit(solution)/shard_map/stack;reshape;reshape | solution.py:223
  169.4 6.6 %copy.46 = bf16[1,2048,1024]{1,2,0:T(8,128)(2,1)} copy(bf16[1,2048,1024]{2,1,0:T(8,128)(2,1)} %stack_reshape_reshape.6) | data formatting | bytes 8388608 | tf_op jit(solution)/shard_map/stack;reshape;reshape | solution.py:223
  176.0 7.4 %stack_reshape_reshape.7 = bf16[1,2048,1024]{2,1,0:T(8,128)(2,1)} reshape(bf16[16,1024,128]{2,1,0:T(8,128)(2,1)} %get-tuple-element.7) | data formatting | bytes 8388608 | tf_op jit(solution)/shard_map/stack;reshape;reshape | solution.py:223
  183.4 6.6 %copy.47 = bf16[1,2048,1024]{1,2,0:T(8,128)(2,1)} copy(bf16[1,2048,1024]{2,1,0:T(8,128)(2,1)} %stack_reshape_reshape.7) | data formatting | bytes 8388608 | tf_op jit(solution)/shard_map/stack;reshape;reshape | solution.py:223
  189.9 6.3 %copy.48 = bf16[1024,16,128]{0,2,1:T(8,128)(2,1)} copy(bf16[1024,16,128]{2,0,1:T(8,128)(2,1)} %get-tuple-element.6) | data formatting | bytes 8388608 | tf_op jit(solution)/shard_map/transpose | solution.py:51
  196.3 28.4 %all-reduce.2.cloned.1.call-done = bf16[1024,2048]{1,0:T(8,128)(2,1)} async-done(((bf16[1024,2048]{1,0:T(8,128)(2,1)}), bf16[1024,2048]{1,0:T(8,128)(2,1)}) %all-reduce.2.cloned.1.call-update) | async-done | bytes 4194320 | tf_op jit(solution)/shard_map/psum | solution.py:214
  224.6 5.6 %fusion = (f32[1024]{0:T(1024)S(1)}, bf16[1024,2048]{1,0:T(8,128)(2,1)S(1)}) fusion(bf16[1024,2048]{1,0:T(8,128)(2,1)} %all-reduce.2.cloned.1.call-done, bf16[1024,2048]{1,0:T(8,128)(2,1)} %all-gather.4.cloned.1.call-done), kind=kLoop, calls=%fused_computation.5 | loop fusion | flops 14679040 | bytes 12587008 | tf_op jit(solution)/shard_map/reduce_sum | solution.py:19
  230.2 0.0 copy-start.1
  230.3 0.0 copy-done.2
  230.3 0.3 copy-done.3
  230.5 11.8 %fusion.21 = f32[2,1024,1024]{1,2,0:T(8,128)} fusion(bf16[1024,2048]{1,0:T(8,128)(2,1)S(1)} %get-tuple-element.4, f32[2048]{0:T(1024)S(1)} %convert_element_type.83, f32[1024]{0:T(1024)S(1)} %add_rsqrt_fusion, bf16[1,2048,1024]{1,2,0:T(8,128)(2,1)S(1)} %copy-done.3, bf16[1,2048,1024]{1,2,0:T(8,128)(2,1)S(1)} %copy-done.2), kind=kOutput, calls=%fused_computation.32 | convolution fusion | flops 8602517504 | bytes 20983808 | tf_op jit(solution)/shard_map/nd,kdf->knf/dot_general | solution.py:220
  242.3 0.0 copy-done.1
  242.3 0.0 copy-done.4
  242.3 9.9 %convolution_convert_fusion.1 = bf16[1024,2048]{1,0:T(8,128)(2,1)} fusion(bf16[1024,2048]{0,1:T(8,128)(2,1)S(1)} %bitcast.71, f32[2,1024,1024]{1,2,0:T(8,128)} %fusion.21), kind=kOutput, calls=%fused_computation.31 | convolution fusion | flops 4303355904 | bytes 16777216 | tf_op jit(solution)/shard_map/dot_general | solution.py:227
  252.2 0.0 reduce-scatter.2.cloned.1.call-update
  252.2 38.1 %reduce-scatter.2.cloned.1.call-done = bf16[1024,256]{1,0:T(8,128)(2,1)} async-done(((bf16[1024,2048]{1,0:T(8,128)(2,1)}), bf16[1024,256]{1,0:T(8,128)(2,1)}) %reduce-scatter.2.cloned.1.call-update) | async-done | bytes 524304 | tf_op jit(solution)/shard_map/reduce_scatter | solution.py:230
  290.4 2.1 add_convert_fusion
  (13 shorter events, 0.0 us)
Async XLA Ops:
  7.2 5.0 %copy-start.6 = (bf16[3,128,256]{2,1,0:T(8,128)(2,1)S(1)}, bf16[3,128,256]{2,1,0:T(8,128)(2,1)}, u32[]{:S(2)}) copy-start(bf16[3,128,256]{2,1,0:T(8,128)(2,1)} %param.12) | copy-start | bytes 589828
  7.2 10.6 %copy-start.7 = (bf16[2048]{0:T(1024)(128)(2,1)S(1)}, bf16[2048]{0:T(1024)(128)(2,1)}, u32[]{:S(2)}) copy-start(bf16[2048]{0:T(1024)(128)(2,1)} %param.14) | copy-start | bytes 12292
  7.2 41.0 %all-gather.4.cloned.1.call-start = ((), (), s32[]{:S(2)}) async-start(), calls=%async_computation.1 | async-start | bytes 4718592 | tf_op jit(solution)/shard_map/all_gather | solution.py:171
  7.9 139.2 %all-gather.6.cloned.1.call-start = ((), (), s32[]{:S(2)}) async-start(), calls=%async_computation.4 | async-start | bytes 14483456 | tf_op jit(solution)/shard_map/all_gather | solution.py:45
  12.1 212.5 %all-reduce.2.cloned.1.call-start = ((), (), s32[]{:S(2)}) async-start(), calls=%async_computation.2 | async-start | bytes 8388608 | tf_op jit(solution)/shard_map/psum | solution.py:214
  12.3 12.6 %collective-permute-start = (bf16[3,128,256]{1,2,0:T(8,128)(2,1)S(1)}, bf16[3,128,256]{1,2,0:T(8,128)(2,1)S(1)}, u32[]{:S(2)}, u32[]{:S(2)}) collective-permute-start(bf16[3,128,256]{1,2,0:T(8,128)(2,1)S(1)} %copy.37), channel_id=1, source_target_pairs={{0,24},{8,0},{16,8},{24,16},{32,56},{40,32},{48,40},{56,48},{64,88... | collective-permute-start | bytes 589832 | tf_op jit(solution)/shard_map/ppermute | solution.py:35
  16.5 9.3 %collective-permute-start.1 = (bf16[3,128,256]{1,2,0:T(8,128)(2,1)S(1)}, bf16[3,128,256]{1,2,0:T(8,128)(2,1)S(1)}, u32[]{:S(2)}, u32[]{:S(2)}) collective-permute-start(bf16[3,128,256]{1,2,0:T(8,128)(2,1)S(1)} %copy.37), channel_id=1, source_target_pairs={{0,16},{8,24},{16,0},{24,8},{32,48},{40,56},{48,32},{56,40},{64,80... | collective-permute-start | bytes 589832 | tf_op jit(solution)/shard_map/ppermute | solution.py:35
  16.5 11.8 %collective-permute-start.2 = (bf16[3,128,256]{1,2,0:T(8,128)(2,1)S(1)}, bf16[3,128,256]{1,2,0:T(8,128)(2,1)S(1)}, u32[]{:S(2)}, u32[]{:S(2)}) collective-permute-start(bf16[3,128,256]{1,2,0:T(8,128)(2,1)S(1)} %copy.37), channel_id=1, source_target_pairs={{0,8},{8,16},{16,24},{24,0},{32,40},{40,48},{48,56},{56,32},{64,72... | collective-permute-start | bytes 589832 | tf_op jit(solution)/shard_map/ppermute | solution.py:35
  28.4 42.2 %collective-permute-start.3 = (bf16[3,4,128,256]{2,3,1,0:T(8,128)(2,1)S(1)}, bf16[3,4,128,256]{2,3,1,0:T(8,128)(2,1)S(1)}, u32[]{:S(2)}, u32[]{:S(2)}) collective-permute-start(bf16[3,4,128,256]{2,3,1,0:T(8,128)(2,1)S(1)} %get-tuple-element.11), channel_id=1, source_target_pairs={{0,96},{8,104},{16,112},{24,120},{32,0},{40,8},{48,16},{56,24},{64... | collective-permute-start | bytes 2359304 | tf_op jit(solution)/shard_map/ppermute | solution.py:37
  31.5 39.2 %collective-permute-start.4 = (bf16[3,4,128,256]{2,3,1,0:T(8,128)(2,1)S(1)}, bf16[3,4,128,256]{2,3,1,0:T(8,128)(2,1)}, u32[]{:S(2)}, u32[]{:S(2)}) collective-permute-start(bf16[3,4,128,256]{2,3,1,0:T(8,128)(2,1)S(1)} %get-tuple-element.11), channel_id=1, source_target_pairs={{0,64},{8,72},{16,80},{24,88},{32,96},{40,104},{48,112},{56,120},{... | collective-permute-start | bytes 2359304 | tf_op jit(solution)/shard_map/ppermute | solution.py:37
  32.1 40.0 %collective-permute-start.5 = (bf16[3,4,128,256]{2,3,1,0:T(8,128)(2,1)S(1)}, bf16[3,4,128,256]{2,3,1,0:T(8,128)(2,1)}, u32[]{:S(2)}, u32[]{:S(2)}) collective-permute-start(bf16[3,4,128,256]{2,3,1,0:T(8,128)(2,1)S(1)} %get-tuple-element.11), channel_id=1, source_target_pairs={{0,32},{8,40},{16,48},{24,56},{32,64},{40,72},{48,80},{56,88},{64,... | collective-permute-start | bytes 2359304 | tf_op jit(solution)/shard_map/ppermute | solution.py:37
  48.2 3.4 %copy-start = (bf16[1024,2048]{1,0:T(8,128)(2,1)S(1)}, bf16[1024,2048]{1,0:T(8,128)(2,1)}, u32[]{:S(2)}) copy-start(bf16[1024,2048]{1,0:T(8,128)(2,1)} %all-gather.4.cloned.1.call-done) | copy-start | bytes 12582916
  143.1 5.8 %copy-start.5 = (bf16[1024,256]{1,0:T(8,128)(2,1)S(1)}, bf16[1024,256]{1,0:T(8,128)(2,1)}, u32[]{:S(2)}) copy-start(bf16[1024,256]{1,0:T(8,128)(2,1)} %shard_map.130) | copy-start | bytes 1572868
  152.3 0.7 copy-start.8
  152.3 138.1 %reduce-scatter.2.cloned.1.call-start = ((), (), s32[]{:S(2)}) async-start(), calls=%async_computation.3 | async-start | bytes 4718592 | tf_op jit(solution)/shard_map/reduce_scatter | solution.py:230
  224.6 5.6 %copy-start.2 = (bf16[1,2048,1024]{1,2,0:T(8,128)(2,1)S(1)}, bf16[1,2048,1024]{1,2,0:T(8,128)(2,1)}, u32[]{:S(2)}) copy-start(bf16[1,2048,1024]{1,2,0:T(8,128)(2,1)} %copy.46) | copy-start | bytes 12582916
  224.6 5.9 %copy-start.3 = (bf16[1,2048,1024]{1,2,0:T(8,128)(2,1)S(1)}, bf16[1,2048,1024]{1,2,0:T(8,128)(2,1)}, u32[]{:S(2)}) copy-start(bf16[1,2048,1024]{1,2,0:T(8,128)(2,1)} %copy.47) | copy-start | bytes 12582916
  230.2 12.1 %copy-start.1 = (bf16[1024,2048]{1,0:T(8,128)(2,1)}, bf16[1024,2048]{1,0:T(8,128)(2,1)S(1)}, u32[]{:S(2)}) copy-start(bf16[1024,2048]{1,0:T(8,128)(2,1)S(1)} %get-tuple-element.4) | copy-start | bytes 12582916
  230.5 11.8 %copy-start.4 = (bf16[1024,16,128]{0,2,1:T(8,128)(2,1)S(1)}, bf16[1024,16,128]{0,2,1:T(8,128)(2,1)}, u32[]{:S(2)}) copy-start(bf16[1024,16,128]{0,2,1:T(8,128)(2,1)} %copy.48) | copy-start | bytes 12582916
Sparse Core Ops, SparseCore 0:
  9.7 38.4 all-gather.3
  50.4 96.6 all-gather.5
  152.4 72.1 all-reduce.1
  252.4 37.9 reduce-scatter.1
